TPU v7x, 512 devices: a whole 4x4x16 slice. The times are simulated.
512 devices in a mesh: expert: 128 (over x, z, core), dp: 4 (over y).
Axes of the slice: x: 4, y: 4, z: 16, core: 2. Of those that a mesh axis runs over, the one named last changes fastest.
Arguments:
- tokens: bfloat16 [16384, 3584], P('expert', 'dp'), may hold values from -6 to 6
- route_ids: int32 [16384, 8], P('expert'), may hold values from 0 to 127, as said below
- gate_scores: float32 [16384, 8], P('expert'), may hold values from 0.1 to 1, as said below
- up_weight: bfloat16 [128, 3584, 1024], P('expert', 'dp'), may hold values from -0.09375 to 0.09375
- down_weight: bfloat16 [128, 1024, 3584], P('expert', None, 'dp'), may hold values from -0.1875 to 0.1875
Outputs:
- mixed: bfloat16 [16384, 3584], P('expert', 'dp')
Inputs may be any that keep to these rules, and one draw needn't show every extreme that they name: `route_ids`: each row names 8 different experts. The same 2 experts are named by exactly 15 rows in every aligned block of 128 rows (the tokens of one device); in such a block every other expert is named by 8 - 1 or 8 rows. `gate_scores`: positive affinities.
All inputs are finite; a program needn't handle non-finite values.
Results may differ from a plain program's by a relative error of at most 0.017.
Values may be sent and summed in bfloat16 or wider, within the bound.
No kernel may reach another device: no remote copies, remote signals or barrier semaphores. Data moves between devices by JAX's collectives and lax.ppermute only.
A program may use at most 64 MiB of HBM per device.

v0:
```python
import jax
import jax.numpy as jnp
from jax import lax
from jax.sharding import PartitionSpec as P

HOT = 2


ROUTE_SCALE = 2.5


def silu_hidden(before):
    summed = lax.psum(before.astype(jnp.bfloat16), "dp").astype(jnp.float32)
    result = jax.nn.silu(summed).astype(jnp.bfloat16)
    return result


def local(tokens, route_ids, gate_scores, up_weight, down_weight):
    token_count, chosen_count = route_ids.shape
    features = tokens.shape[1]
    experts = lax.axis_size("expert")
    mean_rows = token_count * chosen_count // experts
    hot_most = min(2 * mean_rows - 1, token_count)
    cold_rows = (experts - HOT) * mean_rows - HOT * (hot_most - mean_rows)
    cold_most = -(-cold_rows // (experts - HOT))
    flat_ids = route_ids.reshape(-1)
    row_total = flat_ids.shape[0]
    expert_range = jnp.arange(experts, dtype=jnp.int32)
    onehot = (flat_ids[:, None] == expert_range[None, :]).astype(jnp.int32)
    running = jnp.cumsum(onehot, axis=0) - 1
    row_ranks = jnp.sum(onehot * running, axis=1)
    padded = jnp.concatenate([tokens, jnp.zeros((1, features), tokens.dtype)], axis=0)
    up_local = up_weight[0]
    down_local = down_weight[0]
    mix_weights = gate_scores * (ROUTE_SCALE / jnp.sum(gate_scores, axis=1, keepdims=True))
    slot_count = max(hot_most, cold_most)
    slot_of_row = flat_ids * slot_count + row_ranks
    slot_table = jnp.full((experts * slot_count,), row_total, jnp.int32)
    slot_table = slot_table.at[slot_of_row].set(jnp.arange(row_total, dtype=jnp.int32), mode="drop")
    sending = padded[slot_table // chosen_count].reshape(experts, slot_count, features)
    arrived = lax.all_to_all(sending, "expert", split_axis=0, concat_axis=0, tiled=True)
    item_count = arrived.shape[1]
    flat_rows = arrived.reshape(-1, features)
    before = jnp.dot(flat_rows, up_local, preferred_element_type=jnp.float32)
    hidden = silu_hidden(before)
    output = jnp.dot(hidden, down_local, preferred_element_type=jnp.float32)
    outcome = output.astype(jnp.bfloat16).reshape(experts, item_count, features)
    returned = lax.all_to_all(outcome, "expert", split_axis=0, concat_axis=0, tiled=True).reshape(
        -1, features
    )
    picked = returned[slot_of_row]
    picked = picked.reshape(token_count, chosen_count, features).astype(jnp.float32)
    mixed = jnp.sum(mix_weights[:, :, None] * picked, axis=1)
    return mixed.astype(jnp.bfloat16)


def solution(mesh):
    return jax.shard_map(
        local,
        mesh=mesh,
        in_specs=(
            P("expert", "dp"),
            P("expert", None),
            P("expert", None),
            P("expert", "dp", None),
            P("expert", None, "dp"),
        ),
        out_specs=P("expert", "dp"),
        check_vma=False,
    )
```

profile of v0, /device:TPU:1, one launch (start us, length us, event | category | flops | bytes accessed | tf_op | source)
XLA Modules:
  0.0 545.3 jit_solution(15374421908658761649)
XLA Ops:
  6.5 0.0 copy-start
  6.5 0.0 copy-start.1
  6.5 0.0 all-reduce.3.cloned.1.call-start
  6.5 0.9 copy.9
  7.5 0.1 eq.29
  7.6 0.1 eq.25
  7.7 0.7 broadcast_multiply_fusion
  8.4 0.1 copy.11
  8.5 0.2 fusion.14
  8.7 0.1 copy.12
  8.9 0.1 copy.8
  9.0 0.1 mul.44
  9.1 0.4 fusion.13
  9.5 4.3 scatter_custom_fusion
  13.8 0.0 copy-done.1
  13.8 7.1 %gather_fusion = bf16[1920,896]{1,0:T(8,128)(2,1)} fusion(bf16[129,896]{1,0:T(8,128)(2,1)S(1)} %concatenate.3, s32[2048]{0:T(1024)S(1)} %pad_clamp_fusion), kind=kCustom, calls=%fused_computation | custom fusion | bytes 6888960 | tf_op jit(solution)/shard_map/gather | solution.py:40
  21.0 5.7 %reshape.69 = bf16[128,15,896]{2,1,0:T(8,128)(2,1)} reshape(bf16[1920,896]{1,0:T(8,128)(2,1)} %gather_fusion) | data formatting | bytes 6881280 | tf_op jit(solution)/shard_map/reshape | solution.py:40
  26.7 184.9 %all_to_all.10 = bf16[128,15,896]{2,1,0:T(8,128)(2,1)} all-to-all(bf16[128,15,896]{2,1,0:T(8,128)(2,1)} %reshape.69), channel_id=1, replica_groups=mesh['expert'=128,'dp'=4] {'expert'}, dimensions={0} | all-to-all | bytes 6881280 | tf_op jit(solution)/shard_map/all_to_all | solution.py:41
  211.6 5.7 %reshape.70 = bf16[1920,896]{1,0:T(8,128)(2,1)} reshape(bf16[128,15,896]{2,1,0:T(8,128)(2,1)} %all_to_all.10) | data formatting | bytes 6881280 | tf_op jit(solution)/shard_map/reshape | solution.py:43
  217.4 0.0 copy-done
  217.4 7.8 %convolution_convert_fusion = bf16[1920,1024]{1,0:T(8,128)(2,1)} fusion(bf16[1920,896]{1,0:T(8,128)(2,1)} %reshape.70, bf16[1,896,1024]{2,1,0:T(8,128)(2,1)S(1)} %copy-done), kind=kOutput, calls=%fused_computation.11 | convolution fusion | flops 3525181440 | bytes 9207808 | tf_op jit(solution)/shard_map/dot_general | solution.py:44
  225.2 0.0 all-reduce.3.cloned.1.call-update
  225.2 99.6 %all-reduce.3.cloned.1.call-done = bf16[1920,1024]{1,0:T(8,128)(2,1)} async-done(((bf16[1920,1024]{1,0:T(8,128)(2,1)}), bf16[1920,1024]{1,0:T(8,128)(2,1)}) %all-reduce.3.cloned.1.call-update) | async-done | bytes 3932176 | tf_op jit(solution)/shard_map/psum | solution.py:13
  324.8 9.0 %fusion.8 = bf16[1920,896]{1,0:T(8,128)(2,1)} fusion(bf16[1920,1024]{1,0:T(8,128)(2,1)} %all-reduce.3.cloned.1.call-done, bf16[1,1024,896]{2,1,0:T(8,128)(2,1)} %param.9), kind=kOutput, calls=%fused_computation.14 | convolution fusion | flops 3536732160 | bytes 9207808 | tf_op jit(solution)/shard_map/dot_general | solution.py:46
  333.9 5.7 %reshape.71 = bf16[128,15,896]{2,1,0:T(8,128)(2,1)} reshape(bf16[1920,896]{1,0:T(8,128)(2,1)} %fusion.8) | data formatting | bytes 6881280 | tf_op jit(solution)/shard_map/reshape | solution.py:47
  339.6 17.5 %all-to-all-start.1 = ((bf16[128,15,896]{2,1,0:T(8,128)(2,1)}), bf16[128,15,896]{2,1,0:T(8,128)(2,1)}, u32[]{:S(2)}, u32[]{:S(2)}) async-start(bf16[128,15,896]{2,1,0:T(8,128)(2,1)} %reshape.71), calls=%async_computation.1 | async-start | bytes 7340032 | tf_op jit(solution)/shard_map/all_to_all | solution.py:48
  357.1 0.0 copy-done.2
  357.2 0.1 copy.7
  357.3 164.0 %all-to-all-done.1 = bf16[128,15,896]{2,1,0:T(8,128)(2,1)} async-done(((bf16[128,15,896]{2,1,0:T(8,128)(2,1)}), bf16[128,15,896]{2,1,0:T(8,128)(2,1)}, u32[]{:S(2)}, u32[]{:S(2)}) %all-to-all-start.1) | async-done | bytes 3440672 | tf_op jit(solution)/shard_map/all_to_all | solution.py:48
  521.3 5.7 %reshape.72 = bf16[1920,896]{1,0:T(8,128)(2,1)} reshape(bf16[128,15,896]{2,1,0:T(8,128)(2,1)} %all-to-all-done.1) | data formatting | bytes 6881280 | tf_op jit(solution)/shard_map/reshape | solution.py:48
  527.0 8.1 %gather_fusion.1 = bf16[1024,896]{1,0:T(8,128)(2,1)} fusion(bf16[1920,896]{1,0:T(8,128)(2,1)} %reshape.72, s32[1024]{0:T(1024)S(1)} %broadcast_clamp_fusion), kind=kCustom, calls=%fused_computation.1 | custom fusion | bytes 3674112 | tf_op jit(solution)/shard_map/gather | solution.py:51
  535.1 3.4 fusion.7
  (14 shorter events, 0.2 us)
Async XLA Ops:
  6.5 210.8 %copy-start = (bf16[1,896,1024]{2,1,0:T(8,128)(2,1)S(1)}, bf16[1,896,1024]{2,1,0:T(8,128)(2,1)}, u32[]{:S(2)}) copy-start(bf16[1,896,1024]{2,1,0:T(8,128)(2,1)} %param.8) | copy-start | bytes 5505028
  6.5 7.3 %copy-start.1 = (bf16[128,896]{1,0:T(8,128)(2,1)S(1)}, bf16[128,896]{1,0:T(8,128)(2,1)}, u32[]{:S(2)}) copy-start(bf16[128,896]{1,0:T(8,128)(2,1)} %param.5) | copy-start | bytes 688132
  6.5 318.3 %all-reduce.3.cloned.1.call-start = ((), (), s32[]{:S(2)}) async-start(), calls=%async_computation.2 | async-start | bytes 7864320 | tf_op jit(solution)/shard_map/psum | solution.py:13
  339.6 17.5 %copy-start.2 = (f32[128,8]{0,1:T(8,128)S(1)}, f32[128,8]{0,1:T(8,128)}, u32[]{:S(2)}) copy-start(f32[128,8]{0,1:T(8,128)} %param.7) | copy-start | bytes 12292
  339.6 181.7 %all-to-all-start.1 = ((bf16[128,15,896]{2,1,0:T(8,128)(2,1)}), bf16[128,15,896]{2,1,0:T(8,128)(2,1)}, u32[]{:S(2)}, u32[]{:S(2)}) async-start(bf16[128,15,896]{2,1,0:T(8,128)(2,1)} %reshape.71), calls=%async_computation.1 | async-start | bytes 7340032 | tf_op jit(solution)/shard_map/all_to_all | solution.py:48
Sparse Core Ops, SparseCore 0:
  225.3 99.4 all-reduce.2
where the time goes:
time: 548 us; the launch traced here: 545 us
  waiting for transfers between devices  264 us (48%)
  blocking collectives  185 us (34%)
  local copies, waits for them, and re-layouts  44.1 us (8%)
  starting transfers between devices  17.5 us (3%)
  matrix products  16.8 us (3%)
  between operations  13.5 us (2%)
    all_to_all x1, blocking collectives, local(): lax.all_to_all(sending, 'expert', split_axis=0, concat_axis=0, tiled=True)  185 us
    all_to_all x1, waiting for transfers between devices, local(): lax.all_to_all(outcome, 'expert', split_axis=0, concat_axis=0, tiled=True)  164 us
    psum x1, waiting for transfers between devices, silu_hidden(): summed = lax.psum(before.astype(jnp.bfloat16), 'dp').astype(jnp.float32)  99.6 us
    all_to_all x1, starting transfers between devices, local(): lax.all_to_all(outcome, 'expert', split_axis=0, concat_axis=0, tiled=True)  17.5 us
  transfers between devices with their start and end apart: 2, of which 2 were waited for; matrix products, arithmetic and copies ran while one was open for 0% of the time, Pallas kernels for 0%

commit v1 on v0

--- a/solution.py
+++ b/solution.py
@@ -4,6 +4,7 @@
 from jax.sharding import PartitionSpec as P
 
 HOT = 2
+CHUNKS = 3
 
 
 ROUTE_SCALE = 2.5
@@ -13,6 +14,20 @@
     summed = lax.psum(before.astype(jnp.bfloat16), "dp").astype(jnp.float32)
     result = jax.nn.silu(summed).astype(jnp.bfloat16)
     return result
+
+
+def expert_chunk(piece, up_local, down_local, previous):
+    experts, item_count, features = piece.shape
+    arrived = lax.all_to_all(piece, "expert", split_axis=0, concat_axis=0, tiled=True)
+    flat_rows = arrived.reshape(-1, features)
+    before = jnp.dot(flat_rows, up_local, preferred_element_type=jnp.float32)
+    if previous is not None:
+        before, previous = lax.optimization_barrier((before, previous))
+    hidden = silu_hidden(before)
+    output = jnp.dot(hidden, down_local, preferred_element_type=jnp.float32)
+    outcome = output.astype(jnp.bfloat16).reshape(experts, item_count, features)
+    returned = lax.all_to_all(outcome, "expert", split_axis=0, concat_axis=0, tiled=True)
+    return returned, hidden
 
 
 def local(tokens, route_ids, gate_scores, up_weight, down_weight):
@@ -38,16 +53,13 @@
     slot_table = jnp.full((experts * slot_count,), row_total, jnp.int32)
     slot_table = slot_table.at[slot_of_row].set(jnp.arange(row_total, dtype=jnp.int32), mode="drop")
     sending = padded[slot_table // chosen_count].reshape(experts, slot_count, features)
-    arrived = lax.all_to_all(sending, "expert", split_axis=0, concat_axis=0, tiled=True)
-    item_count = arrived.shape[1]
-    flat_rows = arrived.reshape(-1, features)
-    before = jnp.dot(flat_rows, up_local, preferred_element_type=jnp.float32)
-    hidden = silu_hidden(before)
-    output = jnp.dot(hidden, down_local, preferred_element_type=jnp.float32)
-    outcome = output.astype(jnp.bfloat16).reshape(experts, item_count, features)
-    returned = lax.all_to_all(outcome, "expert", split_axis=0, concat_axis=0, tiled=True).reshape(
-        -1, features
-    )
+    bounds = [slot_count * c // CHUNKS for c in range(CHUNKS + 1)]
+    pieces = []
+    previous = None
+    for lo, hi in zip(bounds[:-1], bounds[1:]):
+        returned, previous = expert_chunk(sending[:, lo:hi], up_local, down_local, previous)
+        pieces.append(returned)
+    returned = jnp.concatenate(pieces, axis=1).reshape(-1, features)
     picked = returned[slot_of_row]
     picked = picked.reshape(token_count, chosen_count, features).astype(jnp.float32)
     mixed = jnp.sum(mix_weights[:, :, None] * picked, axis=1)

time: 548 us -> 654 us (1.19)
  waiting for transfers between devices: 264 us -> 319 us
  blocking collectives: 185 us -> 205 us
  starting transfers between devices: 17.5 us -> 37 us
  other arithmetic: 4.75 us -> 14.5 us
    psum x1 -> x3, waiting for transfers between devices: 99.6 us -> 190 us  [silu_hidden(): summed = lax.psum(before.astype(jnp.bfloat16), 'dp').astype(jnp.float32)]
    all_to_all x1 -> x4, waiting for transfers between devices: 164 us -> 129 us  [the longest x3 115 us: expert_chunk(): lax.all_to_all(outcome, 'expert', split_axis=0, concat_axis=0, tiled=True)]
    all_to_all x1 -> x2, blocking collectives: 185 us -> 205 us  [expert_chunk(): lax.all_to_all(piece, 'expert', split_axis=0, concat_axis=0, tiled=True)]
    all_to_all x1 -> x4, starting transfers between devices: 17.5 us -> 36.5 us  [the longest x3 27.4 us: expert_chunk(): lax.all_to_all(outcome, 'expert', split_axis=0, concat_axis=0, tiled=True)]
    dot_general x2 -> x6, matrix products: 16.8 us -> 14.3 us  [the longest x3 7.83 us: expert_chunk(): before = jnp.dot(flat_rows, up_local, preferred_element_type=jnp.float32)]
    reshape x3 -> x7, local copies, waits for them, and re-layouts: 17.1 us -> 17.6 us  [the longest x3 7.39 us: expert_chunk(): flat_rows = arrived.reshape(-1, features)]
  transfers between devices with their start and end apart: 2 -> 7, of which waited for: 2 -> 7; matrix products, arithmetic and copies ran while one was open for 0% -> 5% of each run, Pallas kernels for 0% -> 0%
where the time goes in v1:
time: 654 us; the launch traced here: 653 us
  waiting for transfers between devices  319 us (49%)
  blocking collectives  205 us (31%)
  local copies, waits for them, and re-layouts  50 us (8%)
  starting transfers between devices  37 us (6%)
  other arithmetic  14.5 us (2%)
  matrix products  14.3 us (2%)
  between operations  13.4 us (2%)
    all_to_all x2, blocking collectives, expert_chunk(): lax.all_to_all(piece, 'expert', split_axis=0, concat_axis=0, tiled=True)  205 us
    psum x3, waiting for transfers between devices, silu_hidden(): summed = lax.psum(before.astype(jnp.bfloat16), 'dp').astype(jnp.float32)  190 us
    all_to_all x3, waiting for transfers between devices, expert_chunk(): lax.all_to_all(outcome, 'expert', split_axis=0, concat_axis=0, tiled=True)  115 us
    all_to_all x3, starting transfers between devices, expert_chunk(): lax.all_to_all(outcome, 'expert', split_axis=0, concat_axis=0, tiled=True)  27.4 us
    all_to_all x1, waiting for transfers between devices, expert_chunk(): lax.all_to_all(piece, 'expert', split_axis=0, concat_axis=0, tiled=True)  13.6 us
  transfers between devices with their start and end apart: 7, of which 7 were waited for; matrix products, arithmetic and copies ran while one was open for 5% of the time, Pallas kernels for 0%

profile of v1, /device:TPU:1, one launch (start us, length us, event | category | flops | bytes accessed | tf_op | source)
XLA Modules:
  0.0 652.5 jit_solution(6864148417399794794)
XLA Ops:
  9.4 4.3 scatter_custom_fusion
  13.8 7.1 %gather_fusion = bf16[1920,896]{1,0:T(8,128)(2,1)} fusion(bf16[129,896]{1,0:T(8,128)(2,1)S(1)} %concatenate.6, s32[2048]{0:T(1024)S(1)} %pad_clamp_fusion), kind=kCustom, calls=%fused_computation | custom fusion | bytes 6888960 | tf_op jit(solution)/shard_map/gather | solution.py:55
  21.0 5.7 reshape.81
  26.7 5.4 fusion.48
  32.1 108.1 %all_to_all.30 = bf16[128,5,896]{2,1,0:T(8,128)(2,1)} all-to-all(bf16[128,5,896]{2,1,0:T(8,128)(2,1)S(1)} %get-tuple-element.9), channel_id=1, replica_groups=mesh['expert'=128,'dp'=4] {'expert'}, dimensions={0} | all-to-all | bytes 2293760 | tf_op jit(solution)/shard_map/all_to_all | solution.py:21
  140.2 96.5 %all_to_all.31 = bf16[128,5,896]{2,1,0:T(8,128)(2,1)} all-to-all(bf16[128,5,896]{2,1,0:T(8,128)(2,1)S(1)} %get-tuple-element.11), channel_id=1, replica_groups=mesh['expert'=128,'dp'=4] {'expert'}, dimensions={0} | all-to-all | bytes 2293760 | tf_op jit(solution)/shard_map/all_to_all | solution.py:21
  236.7 9.1 %all-to-all-start.4 = ((bf16[128,5,896]{2,1,0:T(8,128)(2,1)}), bf16[128,5,896]{2,1,0:T(8,128)(2,1)}, u32[]{:S(2)}, u32[]{:S(2)}) async-start(bf16[128,5,896]{2,1,0:T(8,128)(2,1)} %get-tuple-element.10), calls=%async_computation.4 | async-start | bytes 3670016 | tf_op jit(solution)/shard_map/all_to_all | solution.py:21
  246.1 2.5 reshape.82
  248.6 2.6 fusion.25
  251.2 63.4 %all-reduce.5.cloned.1.call-done = bf16[640,1024]{1,0:T(8,128)(2,1)} async-done(((bf16[640,1024]{1,0:T(8,128)(2,1)}), bf16[640,1024]{1,0:T(8,128)(2,1)}) %all-reduce.5.cloned.1.call-update) | async-done | bytes 1310736 | tf_op jit(solution)/shard_map/psum | solution.py:14
  314.6 2.2 fusion.4
  316.8 1.5 fusion.28
  318.3 1.5 reshape.83
  319.8 13.6 %all-to-all-done.4 = bf16[128,5,896]{2,1,0:T(8,128)(2,1)} async-done(((bf16[128,5,896]{2,1,0:T(8,128)(2,1)}), bf16[128,5,896]{2,1,0:T(8,128)(2,1)}, u32[]{:S(2)}, u32[]{:S(2)}) %all-to-all-start.4) | async-done | bytes 1146912 | tf_op jit(solution)/shard_map/all_to_all | solution.py:21
  333.4 9.1 %all-to-all-start.1 = ((bf16[128,5,896]{2,1,0:T(8,128)(2,1)}), bf16[128,5,896]{2,1,0:T(8,128)(2,1)}, u32[]{:S(2)}, u32[]{:S(2)}) async-start(bf16[128,5,896]{2,1,0:T(8,128)(2,1)} %reshape.83), calls=%async_computation.1 | async-start | bytes 3670016 | tf_op jit(solution)/shard_map/all_to_all | solution.py:29
  342.6 2.5 reshape.84
  345.1 2.6 fusion.21
  347.7 63.4 %all-reduce.7.cloned.1.call-done = bf16[640,1024]{1,0:T(8,128)(2,1)} async-done(((bf16[640,1024]{1,0:T(8,128)(2,1)}), bf16[640,1024]{1,0:T(8,128)(2,1)}) %all-reduce.7.cloned.1.call-update) | async-done | bytes 1310736 | tf_op jit(solution)/shard_map/psum | solution.py:14
  411.1 2.2 fusion.8
  416.3 13.8 %all-to-all-done.1 = bf16[128,5,896]{2,1,0:T(8,128)(2,1)} async-done(((bf16[128,5,896]{2,1,0:T(8,128)(2,1)}), bf16[128,5,896]{2,1,0:T(8,128)(2,1)}, u32[]{:S(2)}, u32[]{:S(2)}) %all-to-all-start.1) | async-done | bytes 1146912 | tf_op jit(solution)/shard_map/all_to_all | solution.py:29
  430.1 9.1 %all-to-all-start.3 = ((bf16[128,5,896]{2,1,0:T(8,128)(2,1)}), bf16[128,5,896]{2,1,0:T(8,128)(2,1)}, u32[]{:S(2)}, u32[]{:S(2)}) async-start(bf16[128,5,896]{2,1,0:T(8,128)(2,1)} %reshape.85), calls=%async_computation.3 | async-start | bytes 3670016 | tf_op jit(solution)/shard_map/all_to_all | solution.py:29
  439.5 2.5 reshape.86
  442.0 2.6 fusion.19
  444.6 63.4 %all-reduce.9.cloned.1.call-done = bf16[640,1024]{1,0:T(8,128)(2,1)} async-done(((bf16[640,1024]{1,0:T(8,128)(2,1)}), bf16[640,1024]{1,0:T(8,128)(2,1)}) %all-reduce.9.cloned.1.call-update) | async-done | bytes 1310736 | tf_op jit(solution)/shard_map/psum | solution.py:14
  508.0 3.4 fusion.34
  513.0 13.8 %all-to-all-done.3 = bf16[128,5,896]{2,1,0:T(8,128)(2,1)} async-done(((bf16[128,5,896]{2,1,0:T(8,128)(2,1)}), bf16[128,5,896]{2,1,0:T(8,128)(2,1)}, u32[]{:S(2)}, u32[]{:S(2)}) %all-to-all-start.3) | async-done | bytes 1146912 | tf_op jit(solution)/shard_map/all_to_all | solution.py:29
  526.8 9.1 %all-to-all-start.5 = ((bf16[128,5,896]{2,1,0:T(8,128)(2,1)}), bf16[128,5,896]{2,1,0:T(8,128)(2,1)}, u32[]{:S(2)}, u32[]{:S(2)}) async-start(bf16[128,5,896]{2,1,0:T(8,128)(2,1)} %reshape.87), calls=%async_computation.5 | async-start | bytes 3670016 | tf_op jit(solution)/shard_map/all_to_all | solution.py:29
  536.1 87.4 %all-to-all-done.5 = bf16[128,5,896]{2,1,0:T(8,128)(2,1)} async-done(((bf16[128,5,896]{2,1,0:T(8,128)(2,1)}), bf16[128,5,896]{2,1,0:T(8,128)(2,1)}, u32[]{:S(2)}, u32[]{:S(2)}) %all-to-all-start.5) | async-done | bytes 1146912 | tf_op jit(solution)/shard_map/all_to_all | solution.py:29
  623.5 5.3 pad_maximum_fusion
  628.8 5.7 reshape.88
  634.5 8.1 %gather_fusion.1 = bf16[1024,896]{1,0:T(8,128)(2,1)} fusion(bf16[1920,896]{1,0:T(8,128)(2,1)} %reshape.88, s32[1024]{0:T(1024)S(1)} %broadcast_clamp_fusion), kind=kCustom, calls=%fused_computation.1 | custom fusion | bytes 3674112 | tf_op jit(solution)/shard_map/gather | solution.py:63
  642.6 3.4 fusion
  (43 shorter events, 8.1 us)
Async XLA Ops:
  6.5 242.0 %copy-start = (bf16[1,896,1024]{2,1,0:T(8,128)(2,1)S(1)}, bf16[1,896,1024]{2,1,0:T(8,128)(2,1)}, u32[]{:S(2)}) copy-start(bf16[1,896,1024]{2,1,0:T(8,128)(2,1)} %param.8) | copy-start | bytes 5505028
  7.5 6.3 copy-start.1
  236.7 96.7 %all-to-all-start.4 = ((bf16[128,5,896]{2,1,0:T(8,128)(2,1)}), bf16[128,5,896]{2,1,0:T(8,128)(2,1)}, u32[]{:S(2)}, u32[]{:S(2)}) async-start(bf16[128,5,896]{2,1,0:T(8,128)(2,1)} %get-tuple-element.10), calls=%async_computation.4 | async-start | bytes 3670016 | tf_op jit(solution)/shard_map/all_to_all | solution.py:21
  245.8 68.7 %all-reduce.5.cloned.1.call-start = ((), (), s32[]{:S(2)}) async-start(), calls=%async_computation.6 | async-start | bytes 2621440 | tf_op jit(solution)/shard_map/psum | solution.py:14
  314.6 2.2 copy-start.3
  333.4 96.7 %all-to-all-start.1 = ((bf16[128,5,896]{2,1,0:T(8,128)(2,1)}), bf16[128,5,896]{2,1,0:T(8,128)(2,1)}, u32[]{:S(2)}, u32[]{:S(2)}) async-start(bf16[128,5,896]{2,1,0:T(8,128)(2,1)} %reshape.83), calls=%async_computation.1 | async-start | bytes 3670016 | tf_op jit(solution)/shard_map/all_to_all | solution.py:29
  342.5 68.6 %all-reduce.7.cloned.1.call-start = ((), (), s32[]{:S(2)}) async-start(), calls=%async_computation.7 | async-start | bytes 2621440 | tf_op jit(solution)/shard_map/psum | solution.py:14
  411.1 2.2 copy-start.4
  430.1 96.7 %all-to-all-start.3 = ((bf16[128,5,896]{2,1,0:T(8,128)(2,1)}), bf16[128,5,896]{2,1,0:T(8,128)(2,1)}, u32[]{:S(2)}, u32[]{:S(2)}) async-start(bf16[128,5,896]{2,1,0:T(8,128)(2,1)} %reshape.85), calls=%async_computation.3 | async-start | bytes 3670016 | tf_op jit(solution)/shard_map/all_to_all | solution.py:29
  439.2 68.8 %all-reduce.9.cloned.1.call-start = ((), (), s32[]{:S(2)}) async-start(), calls=%async_computation.8 | async-start | bytes 2621440 | tf_op jit(solution)/shard_map/psum | solution.py:14
  513.0 23.0 %copy-start.2 = (f32[128,8]{0,1:T(8,128)S(1)}, f32[128,8]{0,1:T(8,128)}, u32[]{:S(2)}) copy-start(f32[128,8]{0,1:T(8,128)} %param.7) | copy-start | bytes 12292
  526.8 96.7 %all-to-all-start.5 = ((bf16[128,5,896]{2,1,0:T(8,128)(2,1)}), bf16[128,5,896]{2,1,0:T(8,128)(2,1)}, u32[]{:S(2)}, u32[]{:S(2)}) async-start(bf16[128,5,896]{2,1,0:T(8,128)(2,1)} %reshape.87), calls=%async_computation.5 | async-start | bytes 3670016 | tf_op jit(solution)/shard_map/all_to_all | solution.py:29
Sparse Core Ops, SparseCore 0:
  251.3 63.2 all-reduce.4
  347.8 63.2 all-reduce.6
  444.7 63.2 all-reduce.8

commit v2 on v0

v2 whole, which is shorter than its diff:
```python
import jax
import jax.numpy as jnp
from jax import lax
from jax.sharding import PartitionSpec as P

HOT = 2
ROUTE_SCALE = 2.5
CORES = 2
Z_SIZE = 16
RELAY_OFFSETS = ((0, 0, 0), (0, 0, 1), (0, 1, 0), (0, -1, 0), (1, 0, 0), (-1, 0, 0), (0, 1, 1))


def moved(index, offset, experts, sign):
    x_size = experts // (Z_SIZE * CORES)
    x = index // (Z_SIZE * CORES)
    z = (index // CORES) % Z_SIZE
    c = index % CORES
    dx, dz, dc = offset
    x = (x + sign * dx) % x_size
    z = (z + sign * dz) % Z_SIZE
    c = (c + sign * dc) % CORES
    return (x * Z_SIZE + z) * CORES + c


def silu_hidden(before):
    summed = lax.psum(before.astype(jnp.bfloat16), "dp").astype(jnp.float32)
    result = jax.nn.silu(summed).astype(jnp.bfloat16)
    return result


def local(tokens, route_ids, gate_scores, up_weight, down_weight):
    token_count, chosen_count = route_ids.shape
    features = tokens.shape[1]
    experts = lax.axis_size("expert")
    mean_rows = token_count * chosen_count // experts
    hot_most = min(2 * mean_rows - 1, token_count)
    cold_rows = (experts - HOT) * mean_rows - HOT * (hot_most - mean_rows)
    cold_most = -(-cold_rows // (experts - HOT))
    extra = hot_most - cold_most
    relays = RELAY_OFFSETS[:extra]
    slots = cold_most + HOT
    me = lax.axis_index("expert")

    flat_ids = route_ids.reshape(-1)
    row_total = flat_ids.shape[0]
    expert_range = jnp.arange(experts, dtype=jnp.int32)
    onehot = (flat_ids[:, None] == expert_range[None, :]).astype(jnp.int32)
    running = jnp.cumsum(onehot, axis=0) - 1
    row_ranks = jnp.sum(onehot * running, axis=1)
    counts = jnp.sum(onehot, axis=0)
    _, hot_ids = lax.top_k(counts, HOT)
    hot_ids = hot_ids.astype(jnp.int32)

    is_extra = row_ranks >= cold_most
    hot_slot = jnp.argmax(flat_ids[:, None] == hot_ids[None, :], axis=1).astype(jnp.int32)
    relay_index = jnp.clip(row_ranks - cold_most, 0, extra - 1)
    relay_dest = flat_ids
    for i in range(1, extra):
        relay_dest = jnp.where(relay_index == i, moved(flat_ids, relays[i], experts, 1), relay_dest)
    dest = jnp.where(is_extra, relay_dest, flat_ids)
    slot = jnp.where(is_extra, cold_most + hot_slot, row_ranks)
    position = dest * slots + slot

    padded = jnp.concatenate([tokens, jnp.zeros((1, features), tokens.dtype)], axis=0)
    up_local = up_weight[0]
    down_local = down_weight[0]
    mix_weights = gate_scores * (ROUTE_SCALE / jnp.sum(gate_scores, axis=1, keepdims=True))
    send_table = jnp.full((experts * slots,), row_total, jnp.int32)
    send_table = send_table.at[position].set(jnp.arange(row_total, dtype=jnp.int32), mode="drop")
    sending = padded[send_table // chosen_count].reshape(experts, slots, features)
    arrived = lax.all_to_all(sending, "expert", split_axis=0, concat_axis=0, tiled=True)

    mine = jnp.where(me == hot_ids[0], 0, 1)
    own_extra = jnp.where(mine == 0, arrived[:, cold_most], arrived[:, cold_most + 1])
    hot_rows = [own_extra]
    for i in range(1, extra):
        owner = moved(me, relays[i], experts, -1)
        outgoing = jnp.where(owner == hot_ids[0], arrived[:, cold_most], arrived[:, cold_most + 1])
        pairs = [(int(moved(d, relays[i], experts, 1)), d) for d in range(experts)]
        hot_rows.append(lax.ppermute(outgoing, "expert", pairs))

    flat_rows = jnp.concatenate(
        [arrived[:, :cold_most].reshape(-1, features)] + hot_rows, axis=0
    )
    before = jnp.dot(flat_rows, up_local, preferred_element_type=jnp.float32)
    hidden = silu_hidden(before)
    output = jnp.dot(hidden, down_local, preferred_element_type=jnp.float32)
    outcome = output.astype(jnp.bfloat16)
    regular_count = experts * cold_most
    regular_out = outcome[:regular_count].reshape(experts, cold_most, features)
    hot_out = outcome[regular_count:].reshape(extra, experts, features)

    back = []
    for i in range(1, extra):
        pairs = [(d, int(moved(d, relays[i], experts, 1))) for d in range(experts)]
        back.append(lax.ppermute(hot_out[i], "expert", pairs))
    relay_out = []
    for j in range(HOT):
        result = jnp.where(me == hot_ids[j], hot_out[0], jnp.zeros_like(hot_out[0]))
        for i in range(1, extra):
            owner = moved(me, relays[i], experts, -1)
            result = jnp.where(owner == hot_ids[j], back[i - 1], result)
        relay_out.append(result[:, None])
    outgoing = jnp.concatenate([regular_out] + relay_out, axis=1)
    returned = lax.all_to_all(outgoing, "expert", split_axis=0, concat_axis=0, tiled=True)
    picked = returned.reshape(-1, features)[position]
    picked = picked.reshape(token_count, chosen_count, features).astype(jnp.float32)
    mixed = jnp.sum(mix_weights[:, :, None] * picked, axis=1)
    return mixed.astype(jnp.bfloat16)


def solution(mesh):
    return jax.shard_map(
        local,
        mesh=mesh,
        in_specs=(
            P("expert", "dp"),
            P("expert", None),
            P("expert", None),
            P("expert", "dp", None),
            P("expert", None, "dp"),
        ),
        out_specs=P("expert", "dp"),
        check_vma=False,
    )
```

time: 548 us -> 601 us (1.097)
  blocking collectives: 185 us -> 0 us
  waiting for transfers between devices: 264 us -> 431 us
  starting transfers between devices: 17.5 us -> 76.4 us
  other arithmetic: 4.75 us -> 19 us
  between operations: 13.5 us -> 23.4 us
  local copies, waits for them, and re-layouts: 44.1 us -> 35.8 us
    all_to_all x1 -> x0, blocking collectives: 185 us -> none  [local(): lax.all_to_all(sending, 'expert', split_axis=0, concat_axis=0, tiled=True)]
    all_to_all x1 -> x2, waiting for transfers between devices: 164 us -> 322 us  [the longest x1 164 us: local(): lax.all_to_all(outgoing, 'expert', split_axis=0, concat_axis=0, tiled=True)]
    ppermute x0 -> x12, starting transfers between devices: none -> 38.2 us  [the longest x6 19.3 us: local(): hot_rows.append(lax.ppermute(outgoing, 'expert', pairs))]
    all_to_all x1 -> x2, starting transfers between devices: 17.5 us -> 38.2 us  [the longest x1 20.8 us: local(): lax.all_to_all(sending, 'expert', split_axis=0, concat_axis=0, tiled=True)]
    reshape x4 -> x3, local copies, waits for them, and re-layouts: 22.9 us -> 12.2 us  [the longest x1 5.33 us: local(): picked = returned.reshape(-1, features)[position]]
    ppermute x0 -> x12, waiting for transfers between devices: none -> 9.08 us  [the longest x6 5.82 us: local(): hot_rows.append(lax.ppermute(outgoing, 'expert', pairs))]
    select_n x2 -> x3, other arithmetic: 0.02 us -> 6.54 us  [the longest x2 6.53 us: local(): jnp.where(owner == hot_ids[0], arrived[:, cold_most], arrived[:, cold_mos...]
  transfers between devices with their start and end apart: 2 -> 15, of which waited for: 2 -> 7; matrix products, arithmetic and copies ran while one was open for 0% -> 1% of each run, Pallas kernels for 0% -> 0%
where the time goes in v2:
time: 601 us; the launch traced here: 599 us
  waiting for transfers between devices  431 us (72%)
  starting transfers between devices  76.4 us (13%)
  local copies, waits for them, and re-layouts  35.8 us (6%)
  between operations  23.4 us (4%)
  other arithmetic  19 us (3%)
  matrix products  12.9 us (2%)
    all_to_all x1, waiting for transfers between devices, local(): lax.all_to_all(outgoing, 'expert', split_axis=0, concat_axis=0, tiled=True)  164 us
    all_to_all x1, waiting for transfers between devices, local(): lax.all_to_all(sending, 'expert', split_axis=0, concat_axis=0, tiled=True)  158 us
    psum x1, waiting for transfers between devices, silu_hidden(): summed = lax.psum(before.astype(jnp.bfloat16), 'dp').astype(jnp.float32)  99.5 us
    all_to_all x1, starting transfers between devices, local(): lax.all_to_all(sending, 'expert', split_axis=0, concat_axis=0, tiled=True)  20.8 us
    ppermute x6, starting transfers between devices, local(): hot_rows.append(lax.ppermute(outgoing, 'expert', pairs))  19.3 us
    ppermute x6, starting transfers between devices, local(): back.append(lax.ppermute(hot_out[i], 'expert', pairs))  18.9 us
    all_to_all x1, starting transfers between devices, local(): lax.all_to_all(outgoing, 'expert', split_axis=0, concat_axis=0, tiled=True)  17.4 us
  transfers between devices with their start and end apart: 15, of which 7 were waited for; matrix products, arithmetic and copies ran while one was open for 1% of the time, Pallas kernels for 0%

profile of v2, /device:TPU:1, one launch (start us, length us, event | category | flops | bytes accessed | tf_op | source)
XLA Modules:
  0.0 598.6 jit_solution(8038164619967327586)
XLA Ops:
  8.5 2.5 top_k.11
  11.8 4.3 scatter_custom_fusion
  16.2 5.0 gather_fusion
  21.2 5.2 reshape.71
  26.4 20.8 %all-to-all-start = ((bf16[128,10,896]{2,1,0:T(8,128)(2,1)}), bf16[128,10,896]{2,1,0:T(8,128)(2,1)}, u32[]{:S(2)}, u32[]{:S(2)}) async-start(bf16[128,10,896]{2,1,0:T(8,128)(2,1)} %reshape.71), calls=%async_computation | async-start | bytes 7340032 | tf_op jit(solution)/shard_map/all_to_all | solution.py:71
  52.9 158.4 %all-to-all-done = bf16[128,10,896]{2,1,0:T(8,128)(2,1)} async-done(((bf16[128,10,896]{2,1,0:T(8,128)(2,1)}), bf16[128,10,896]{2,1,0:T(8,128)(2,1)}, u32[]{:S(2)}, u32[]{:S(2)}) %all-to-all-start) | async-done | bytes 2293792 | tf_op jit(solution)/shard_map/all_to_all | solution.py:71
  211.4 2.8 broadcast_select_fusion.5
  214.2 3.7 collective-permute-start
  217.8 3.8 broadcast_select_fusion
  221.6 2.7 collective-permute-start.1
  224.4 3.7 collective-permute-start.2
  228.2 3.2 collective-permute-start.3
  231.4 2.1 collective-permute-start.4
  235.2 4.0 collective-permute-start.5
  241.1 4.1 collective-permute-done.5
  245.2 5.7 convolution_convert_fusion
  251.0 99.5 %all-reduce.3.cloned.1.call-done = bf16[1920,1024]{1,0:T(8,128)(2,1)} async-done(((bf16[1920,1024]{1,0:T(8,128)(2,1)}), bf16[1920,1024]{1,0:T(8,128)(2,1)}) %all-reduce.3.cloned.1.call-update) | async-done | bytes 3932176 | tf_op jit(solution)/shard_map/psum | solution.py:26
  350.5 7.2 %fusion.8 = bf16[1920,896]{1,0:T(8,128)(2,1)S(1)} fusion(bf16[1920,1024]{1,0:T(8,128)(2,1)} %all-reduce.3.cloned.1.call-done, bf16[1,1024,896]{2,1,0:T(8,128)(2,1)} %param.9), kind=kOutput, calls=%fused_computation.15 | convolution fusion | flops 3536732160 | bytes 9207808 | tf_op jit(solution)/shard_map/dot_general | solution.py:87
  357.7 1.7 copy-done.1
  359.6 3.2 collective-permute-start.10
  367.3 3.0 collective-permute-start.11
  370.3 3.1 collective-permute-start.6
  373.4 4.3 collective-permute-start.7
  377.7 1.9 collective-permute-start.8
  379.7 3.3 collective-permute-start.9
  384.7 2.5 collective-permute-done.8
  390.8 3.0 pad_maximum_fusion
  393.8 17.4 %all-to-all-start.1 = ((bf16[128,10,896]{2,1,0:T(8,128)(2,1)}), bf16[128,10,896]{2,1,0:T(8,128)(2,1)}, u32[]{:S(2)}, u32[]{:S(2)}) async-start(bf16[128,10,896]{2,1,0:T(8,128)(2,1)} %pad_maximum_fusion), calls=%async_computation.1 | async-start | bytes 7340032 | tf_op jit(solution)/shard_map/all_to_all | solution.py:105
  411.4 164.0 %all-to-all-done.1 = bf16[128,10,896]{2,1,0:T(8,128)(2,1)} async-done(((bf16[128,10,896]{2,1,0:T(8,128)(2,1)}), bf16[128,10,896]{2,1,0:T(8,128)(2,1)}, u32[]{:S(2)}, u32[]{:S(2)}) %all-to-all-start.1) | async-done | bytes 2293792 | tf_op jit(solution)/shard_map/all_to_all | solution.py:105
  575.4 5.3 reshape.74
  580.7 7.7 %gather_fusion.1 = bf16[1024,896]{1,0:T(8,128)(2,1)} fusion(bf16[1280,896]{1,0:T(8,128)(2,1)} %reshape.74, s32[1024]{0:T(1024)S(1)} %get-tuple-element.13), kind=kCustom, calls=%fused_computation.1 | custom fusion | bytes 3674112 | tf_op jit(solution)/shard_map/gather | solution.py:106
  588.4 3.4 fusion.7
  (62 shorter events, 12.6 us)
Async XLA Ops:
  6.5 238.7 %copy-start = (bf16[1,896,1024]{2,1,0:T(8,128)(2,1)S(1)}, bf16[1,896,1024]{2,1,0:T(8,128)(2,1)}, u32[]{:S(2)}) copy-start(bf16[1,896,1024]{2,1,0:T(8,128)(2,1)} %param.8) | copy-start | bytes 5505028
  6.5 9.6 %copy-start.2 = (bf16[128,896]{1,0:T(8,128)(2,1)S(1)}, bf16[128,896]{1,0:T(8,128)(2,1)}, u32[]{:S(2)}) copy-start(bf16[128,896]{1,0:T(8,128)(2,1)} %param.5) | copy-start | bytes 688132
  26.4 184.9 %all-to-all-start = ((bf16[128,10,896]{2,1,0:T(8,128)(2,1)}), bf16[128,10,896]{2,1,0:T(8,128)(2,1)}, u32[]{:S(2)}, u32[]{:S(2)}) async-start(bf16[128,10,896]{2,1,0:T(8,128)(2,1)} %reshape.71), calls=%async_computation | async-start | bytes 7340032 | tf_op jit(solution)/shard_map/all_to_all | solution.py:71
  47.2 303.3 %all-reduce.3.cloned.1.call-start = ((), (), s32[]{:S(2)}) async-start(), calls=%async_computation.2 | async-start | bytes 7864320 | tf_op jit(solution)/shard_map/psum | solution.py:26
  214.2 21.1 %collective-permute-start = (bf16[128,896]{1,0:T(8,128)(2,1)S(1)}, bf16[128,896]{1,0:T(8,128)(2,1)S(1)}, u32[]{:S(2)}, u32[]{:S(2)}) collective-permute-start(bf16[128,896]{1,0:T(8,128)(2,1)S(1)} %bitcast.51), channel_id=1, source_target_pairs={{4,0},{0,4},{12,8},{8,12},{20,16},{16,20},{28,24},{24,28},{36,32},... | collective-permute-start | bytes 688136 | tf_op jit(solution)/shard_map/ppermute | solution.py:80
  221.6 17.6 %collective-permute-start.1 = (bf16[128,896]{1,0:T(8,128)(2,1)S(1)}, bf16[128,896]{1,0:T(8,128)(2,1)S(1)}, u32[]{:S(2)}, u32[]{:S(2)}) collective-permute-start(bf16[128,896]{1,0:T(8,128)(2,1)S(1)} %bitcast.55), channel_id=1, source_target_pairs={{8,0},{12,4},{16,8},{20,12},{24,16},{28,20},{32,24},{36,28},{40,32... | collective-permute-start | bytes 688136 | tf_op jit(solution)/shard_map/ppermute | solution.py:80
  224.4 14.9 %collective-permute-start.2 = (bf16[128,896]{1,0:T(8,128)(2,1)S(1)}, bf16[128,896]{1,0:T(8,128)(2,1)S(1)}, u32[]{:S(2)}, u32[]{:S(2)}) collective-permute-start(bf16[128,896]{1,0:T(8,128)(2,1)S(1)} %bitcast.54), channel_id=1, source_target_pairs={{120,0},{124,4},{0,8},{4,12},{8,16},{12,20},{16,24},{20,28},{24,32... | collective-permute-start | bytes 688136 | tf_op jit(solution)/shard_map/ppermute | solution.py:80
  228.2 11.2 %collective-permute-start.3 = (bf16[128,896]{1,0:T(8,128)(2,1)S(1)}, bf16[128,896]{1,0:T(8,128)(2,1)S(1)}, u32[]{:S(2)}, u32[]{:S(2)}) collective-permute-start(bf16[128,896]{1,0:T(8,128)(2,1)S(1)} %bitcast.53), channel_id=1, source_target_pairs={{128,0},{132,4},{136,8},{140,12},{144,16},{148,20},{152,24},{156,2... | collective-permute-start | bytes 688136 | tf_op jit(solution)/shard_map/ppermute | solution.py:80
  231.4 9.7 %collective-permute-start.4 = (bf16[128,896]{1,0:T(8,128)(2,1)S(1)}, bf16[128,896]{1,0:T(8,128)(2,1)S(1)}, u32[]{:S(2)}, u32[]{:S(2)}) collective-permute-start(bf16[128,896]{1,0:T(8,128)(2,1)S(1)} %bitcast.52), channel_id=1, source_target_pairs={{384,0},{388,4},{392,8},{396,12},{400,16},{404,20},{408,24},{412,2... | collective-permute-start | bytes 688136 | tf_op jit(solution)/shard_map/ppermute | solution.py:80
  235.2 10.0 %collective-permute-start.5 = (bf16[128,896]{1,0:T(8,128)(2,1)S(1)}, bf16[128,896]{1,0:T(8,128)(2,1)S(1)}, u32[]{:S(2)}, u32[]{:S(2)}) collective-permute-start(bf16[128,896]{1,0:T(8,128)(2,1)S(1)} %bitcast.56), channel_id=1, source_target_pairs={{12,0},{8,4},{20,8},{16,12},{28,16},{24,20},{36,24},{32,28},{44,32... | collective-permute-start | bytes 688136 | tf_op jit(solution)/shard_map/ppermute | solution.py:80
  357.7 1.7 copy-start.1
  359.6 20.1 %collective-permute-start.10 = (bf16[128,896]{1,0:T(8,128)(2,1)S(1)}, bf16[128,896]{1,0:T(8,128)(2,1)S(1)}, u32[]{:S(2)}, u32[]{:S(2)}) collective-permute-start(bf16[128,896]{1,0:T(8,128)(2,1)S(1)} %get-tuple-element.22), channel_id=1, source_target_pairs={{0,8},{4,12},{8,16},{12,20},{16,24},{20,28},{24,32},{28,36},{32,40... | collective-permute-start | bytes 688136 | tf_op jit(solution)/shard_map/ppermute | solution.py:96
  367.3 17.4 %collective-permute-start.11 = (bf16[128,896]{1,0:T(8,128)(2,1)S(1)}, bf16[128,896]{1,0:T(8,128)(2,1)S(1)}, u32[]{:S(2)}, u32[]{:S(2)}) collective-permute-start(bf16[128,896]{1,0:T(8,128)(2,1)S(1)} %get-tuple-element.21), channel_id=1, source_target_pairs={{0,4},{4,0},{8,12},{12,8},{16,20},{20,16},{24,28},{28,24},{32,36},... | collective-permute-start | bytes 688136 | tf_op jit(solution)/shard_map/ppermute | solution.py:96
  370.3 14.4 %collective-permute-start.6 = (bf16[128,896]{1,0:T(8,128)(2,1)S(1)}, bf16[128,896]{1,0:T(8,128)(2,1)S(1)}, u32[]{:S(2)}, u32[]{:S(2)}) collective-permute-start(bf16[128,896]{1,0:T(8,128)(2,1)S(1)} %get-tuple-element.26), channel_id=1, source_target_pairs={{0,12},{4,8},{8,20},{12,16},{16,28},{20,24},{24,36},{28,32},{32,44... | collective-permute-start | bytes 688136 | tf_op jit(solution)/shard_map/ppermute | solution.py:96
  373.4 11.3 %collective-permute-start.7 = (bf16[128,896]{1,0:T(8,128)(2,1)S(1)}, bf16[128,896]{1,0:T(8,128)(2,1)S(1)}, u32[]{:S(2)}, u32[]{:S(2)}) collective-permute-start(bf16[128,896]{1,0:T(8,128)(2,1)S(1)} %get-tuple-element.25), channel_id=1, source_target_pairs={{0,384},{4,388},{8,392},{12,396},{16,400},{20,404},{24,408},{28,41... | collective-permute-start | bytes 688136 | tf_op jit(solution)/shard_map/ppermute | solution.py:96
  377.7 9.5 %collective-permute-start.8 = (bf16[128,896]{1,0:T(8,128)(2,1)S(1)}, bf16[128,896]{1,0:T(8,128)(2,1)S(1)}, u32[]{:S(2)}, u32[]{:S(2)}) collective-permute-start(bf16[128,896]{1,0:T(8,128)(2,1)S(1)} %get-tuple-element.24), channel_id=1, source_target_pairs={{0,128},{4,132},{8,136},{12,140},{16,144},{20,148},{24,152},{28,15... | collective-permute-start | bytes 688136 | tf_op jit(solution)/shard_map/ppermute | solution.py:96
  379.7 8.3 %collective-permute-start.9 = (bf16[128,896]{1,0:T(8,128)(2,1)S(1)}, bf16[128,896]{1,0:T(8,128)(2,1)S(1)}, u32[]{:S(2)}, u32[]{:S(2)}) collective-permute-start(bf16[128,896]{1,0:T(8,128)(2,1)S(1)} %get-tuple-element.23), channel_id=1, source_target_pairs={{0,120},{4,124},{8,0},{12,4},{16,8},{20,12},{24,16},{28,20},{32,24... | collective-permute-start | bytes 688136 | tf_op jit(solution)/shard_map/ppermute | solution.py:96
  393.8 17.4 %copy-start.3 = (f32[128,8]{0,1:T(8,128)S(1)}, f32[128,8]{0,1:T(8,128)}, u32[]{:S(2)}) copy-start(f32[128,8]{0,1:T(8,128)} %param.7) | copy-start | bytes 12292
  393.8 181.6 %all-to-all-start.1 = ((bf16[128,10,896]{2,1,0:T(8,128)(2,1)}), bf16[128,10,896]{2,1,0:T(8,128)(2,1)}, u32[]{:S(2)}, u32[]{:S(2)}) async-start(bf16[128,10,896]{2,1,0:T(8,128)(2,1)} %pad_maximum_fusion), calls=%async_computation.1 | async-start | bytes 7340032 | tf_op jit(solution)/shard_map/all_to_all | solution.py:105
Sparse Core Ops, SparseCore 0:
  251.1 99.3 all-reduce.2

commit v3 on v2

--- a/solution.py
+++ b/solution.py
@@ -20,6 +20,14 @@
     z = (z + sign * dz) % Z_SIZE
     c = (c + sign * dc) % CORES
     return (x * Z_SIZE + z) * CORES + c
+
+
+def exchange(rows, experts):
+    shape = rows.shape
+    tile_rows = 8
+    packed = rows.reshape(experts * tile_rows, -1)
+    moved_rows = lax.all_to_all(packed, "expert", split_axis=0, concat_axis=0, tiled=True)
+    return moved_rows.reshape(shape)
 
 
 def silu_hidden(before):
@@ -67,8 +75,8 @@
     mix_weights = gate_scores * (ROUTE_SCALE / jnp.sum(gate_scores, axis=1, keepdims=True))
     send_table = jnp.full((experts * slots,), row_total, jnp.int32)
     send_table = send_table.at[position].set(jnp.arange(row_total, dtype=jnp.int32), mode="drop")
-    sending = padded[send_table // chosen_count].reshape(experts, slots, features)
-    arrived = lax.all_to_all(sending, "expert", split_axis=0, concat_axis=0, tiled=True)
+    sending = padded[send_table // chosen_count]
+    arrived = exchange(sending, experts).reshape(experts, slots, features)
 
     mine = jnp.where(me == hot_ids[0], 0, 1)
     own_extra = jnp.where(mine == 0, arrived[:, cold_most], arrived[:, cold_most + 1])
@@ -102,7 +110,7 @@
             result = jnp.where(owner == hot_ids[j], back[i - 1], result)
         relay_out.append(result[:, None])
     outgoing = jnp.concatenate([regular_out] + relay_out, axis=1)
-    returned = lax.all_to_all(outgoing, "expert", split_axis=0, concat_axis=0, tiled=True)
+    returned = exchange(outgoing, experts)
     picked = returned.reshape(-1, features)[position]
     picked = picked.reshape(token_count, chosen_count, features).astype(jnp.float32)
     mixed = jnp.sum(mix_weights[:, :, None] * picked, axis=1)

time: 601 us -> 512 us (0.85)
  waiting for transfers between devices: 431 us -> 314 us
  local copies, waits for them, and re-layouts: 35.8 us -> 71 us
    all_to_all x2, waiting for transfers between devices: 322 us -> 214 us  [exchange(): lax.all_to_all(packed, 'expert', split_axis=0, concat_axis=0, tiled=True)]
    all_to_all x0 -> x3, local copies, waits for them, and re-layouts: none -> 15 us  [exchange(): lax.all_to_all(packed, 'expert', split_axis=0, concat_axis=0, tiled=True)]
    reshape x2 -> x0, local copies, waits for them, and re-layouts: 10.6 us -> none  [the longest x1 5.33 us: local(): picked = returned.reshape(-1, features)[position]]
    unnamed x22 -> x16, local copies, waits for them, and re-layouts: 4.68 us -> 12.7 us
    slice x0 -> x2, local copies, waits for them, and re-layouts: none -> 6.8 us  [local(): arrived[:, :cold_most].reshape(-1, features)]
    another operation x2 -> x3, local copies, waits for them, and re-layouts: 0.01 us -> 6.5 us  [the longest x1 6.49 us: local(): picked = returned.reshape(-1, features)[position]]
  transfers between devices with their start and end apart: 15 -> 15, of which waited for: 7 -> 5; matrix products, arithmetic and copies ran while one was open for 1% -> 5% of each run, Pallas kernels for 0% -> 0%
where the time goes in v3:
time: 512 us; the launch traced here: 510 us
  waiting for transfers between devices  314 us (61%)
  starting transfers between devices  72.9 us (14%)
  local copies, waits for them, and re-layouts  71 us (14%)
  between operations  22.8 us (4%)
  matrix products  15 us (3%)
  other arithmetic  14.8 us (3%)
    all_to_all x2, waiting for transfers between devices, exchange(): lax.all_to_all(packed, 'expert', split_axis=0, concat_axis=0, tiled=True)  214 us
    psum x1, waiting for transfers between devices, silu_hidden(): summed = lax.psum(before.astype(jnp.bfloat16), 'dp').astype(jnp.float32)  97.1 us
    all_to_all x2, starting transfers between devices, exchange(): lax.all_to_all(packed, 'expert', split_axis=0, concat_axis=0, tiled=True)  35.5 us
    ppermute x6, starting transfers between devices, local(): back.append(lax.ppermute(hot_out[i], 'expert', pairs))  18.7 us
    ppermute x6, starting transfers between devices, local(): hot_rows.append(lax.ppermute(outgoing, 'expert', pairs))  18.6 us
    all_to_all x3, local copies, waits for them, and re-layouts, exchange(): lax.all_to_all(packed, 'expert', split_axis=0, concat_axis=0, tiled=True)  15 us
    unnamed x16, local copies, waits for them, and re-layouts  12.7 us
  transfers between devices with their start and end apart: 15, of which 5 were waited for; matrix products, arithmetic and copies ran while one was open for 5% of the time, Pallas kernels for 0%

profile of v3, /device:TPU:1, one launch (start us, length us, event | category | flops | bytes accessed | tf_op | source)
XLA Modules:
  0.0 510.3 jit_solution(6677949570908917772)
XLA Ops:
  8.5 2.5 top_k.11
  11.8 4.3 scatter_custom_fusion
  16.2 5.0 gather_fusion
  21.2 6.0 %all_to_all.12 = bf16[128,8,1120]{2,1,0:T(8,128)(2,1)} reshape(bf16[1280,896]{1,0:T(8,128)(2,1)} %gather_fusion) | data formatting | bytes 4587520 | tf_op jit(solution)/shard_map/all_to_all | solution.py:29
  27.2 20.8 %all-to-all-start = ((bf16[128,8,1120]{2,1,0:T(8,128)(2,1)}), bf16[128,8,1120]{2,1,0:T(8,128)(2,1)}, u32[]{:S(2)}, u32[]{:S(2)}) async-start(bf16[128,8,1120]{2,1,0:T(8,128)(2,1)} %all_to_all.12), calls=%async_computation | async-start | bytes 4718592 | tf_op jit(solution)/shard_map/all_to_all | solution.py:29
  53.4 104.4 %all-to-all-done = bf16[128,8,1120]{2,1,0:T(8,128)(2,1)} async-done(((bf16[128,8,1120]{2,1,0:T(8,128)(2,1)}), bf16[128,8,1120]{2,1,0:T(8,128)(2,1)}, u32[]{:S(2)}, u32[]{:S(2)}) %all-to-all-start) | async-done | bytes 2293792 | tf_op jit(solution)/shard_map/all_to_all | solution.py:29
  157.8 4.5 copy.67
  162.3 2.9 slice.117
  169.5 3.9 copy.68
  176.1 3.3 collective-permute-start.4
  179.4 3.2 collective-permute-start.3
  182.6 3.9 collective-permute-start.2
  186.5 2.6 collective-permute-start.1
  189.1 2.9 bitcast_dynamic-update-slice_fusion
  192.9 3.1 collective-permute-start.5
  203.4 7.8 %convolution_convert_fusion = bf16[1920,1024]{1,0:T(8,128)(2,1)} fusion(bf16[1920,896]{1,0:T(8,128)(2,1)} %constant_dynamic-update-slice_fusion, bf16[1,896,1024]{2,1,0:T(8,128)(2,1)S(1)} %copy-done), kind=kOutput, calls=%fused_computation.11 | convolution fusion | flops 3525181440 | bytes 9207808 | tf_op jit(solution)/shard_map/dot_general | solution.py:93
  211.2 97.1 %all-reduce.3.cloned.1.call-done = bf16[1920,1024]{1,0:T(8,128)(2,1)} async-done(((bf16[1920,1024]{1,0:T(8,128)(2,1)}), bf16[1920,1024]{1,0:T(8,128)(2,1)}) %all-reduce.3.cloned.1.call-update) | async-done | bytes 3932176 | tf_op jit(solution)/shard_map/psum | solution.py:34
  308.3 7.2 %fusion.8 = bf16[1920,896]{1,0:T(8,128)(2,1)S(1)} fusion(bf16[1920,1024]{1,0:T(8,128)(2,1)} %all-reduce.3.cloned.1.call-done, bf16[1,1024,896]{2,1,0:T(8,128)(2,1)} %param.9), kind=kOutput, calls=%fused_computation.14 | convolution fusion | flops 3536732160 | bytes 9207808 | tf_op jit(solution)/shard_map/dot_general | solution.py:95
  318.2 2.7 collective-permute-start.11
  325.3 3.2 collective-permute-start.10
  328.5 4.4 collective-permute-start.9
  332.9 3.1 collective-permute-start.8
  336.0 3.4 collective-permute-start.7
  341.4 2.9 slice_bitcast_fusion
  344.3 3.8 copy.76
  353.6 3.3 pad_maximum_fusion
  356.9 4.5 copy.79
  361.4 14.7 %all-to-all-start.1 = ((bf16[128,8,1120]{2,1,0:T(8,128)(2,1)}), bf16[128,8,1120]{2,1,0:T(8,128)(2,1)}, u32[]{:S(2)}, u32[]{:S(2)}) async-start(bf16[128,8,1120]{2,1,0:T(8,128)(2,1)} %copy.79), calls=%async_computation.1 | async-start | bytes 4718592 | tf_op jit(solution)/shard_map/all_to_all | solution.py:29
  376.3 109.6 %all-to-all-done.1 = bf16[128,8,1120]{2,1,0:T(8,128)(2,1)} async-done(((bf16[128,8,1120]{2,1,0:T(8,128)(2,1)}), bf16[128,8,1120]{2,1,0:T(8,128)(2,1)}, u32[]{:S(2)}, u32[]{:S(2)}) %all-to-all-start.1) | async-done | bytes 2293792 | tf_op jit(solution)/shard_map/all_to_all | solution.py:29
  485.9 6.5 %reshape_reshape.7 = bf16[1280,896]{1,0:T(8,128)(2,1)} reshape(bf16[128,8,1120]{2,1,0:T(8,128)(2,1)} %all-to-all-done.1) | data formatting | bytes 4587520 | tf_op jit(solution)/shard_map/reshape;reshape | solution.py:114
  492.4 7.7 %gather_fusion.1 = bf16[1024,896]{1,0:T(8,128)(2,1)} fusion(bf16[1280,896]{1,0:T(8,128)(2,1)} %reshape_reshape.7, s32[1024]{0:T(1024)S(1)} %get-tuple-element.13), kind=kCustom, calls=%fused_computation.1 | custom fusion | bytes 3674112 | tf_op jit(solution)/shard_map/gather | solution.py:114
  500.1 3.4 fusion.7
  (68 shorter events, 28.8 us)
Async XLA Ops:
  6.5 196.8 %copy-start = (bf16[1,896,1024]{2,1,0:T(8,128)(2,1)S(1)}, bf16[1,896,1024]{2,1,0:T(8,128)(2,1)}, u32[]{:S(2)}) copy-start(bf16[1,896,1024]{2,1,0:T(8,128)(2,1)} %param.8) | copy-start | bytes 5505028
  6.5 9.6 %copy-start.2 = (bf16[128,896]{1,0:T(8,128)(2,1)S(1)}, bf16[128,896]{1,0:T(8,128)(2,1)}, u32[]{:S(2)}) copy-start(bf16[128,896]{1,0:T(8,128)(2,1)} %param.5) | copy-start | bytes 688132
  27.2 130.6 %all-to-all-start = ((bf16[128,8,1120]{2,1,0:T(8,128)(2,1)}), bf16[128,8,1120]{2,1,0:T(8,128)(2,1)}, u32[]{:S(2)}, u32[]{:S(2)}) async-start(bf16[128,8,1120]{2,1,0:T(8,128)(2,1)} %all_to_all.12), calls=%async_computation | async-start | bytes 4718592 | tf_op jit(solution)/shard_map/all_to_all | solution.py:29
  48.0 260.3 %all-reduce.3.cloned.1.call-start = ((), (), s32[]{:S(2)}) async-start(), calls=%async_computation.2 | async-start | bytes 7864320 | tf_op jit(solution)/shard_map/psum | solution.py:34
  167.1 25.8 %collective-permute-start = (bf16[128,896]{1,0:T(8,128)(2,1)}, bf16[128,896]{1,0:T(8,128)(2,1)S(1)}, u32[]{:S(2)}, u32[]{:S(2)}) collective-permute-start(bf16[128,896]{1,0:T(8,128)(2,1)} %bitcast.7), channel_id=1, source_target_pairs={{4,0},{0,4},{12,8},{8,12},{20,16},{16,20},{28,24},{24,28},{36,32},... | collective-permute-start | bytes 688136 | tf_op jit(solution)/shard_map/ppermute | solution.py:88
  176.1 25.6 %collective-permute-start.4 = (bf16[128,896]{1,0:T(8,128)(2,1)S(1)}, bf16[128,896]{1,0:T(8,128)(2,1)S(1)}, u32[]{:S(2)}, u32[]{:S(2)}) collective-permute-start(bf16[128,896]{1,0:T(8,128)(2,1)S(1)} %bitcast.44), channel_id=1, source_target_pairs={{384,0},{388,4},{392,8},{396,12},{400,16},{404,20},{408,24},{412,2... | collective-permute-start | bytes 688136 | tf_op jit(solution)/shard_map/ppermute | solution.py:88
  179.4 20.7 %collective-permute-start.3 = (bf16[128,896]{1,0:T(8,128)(2,1)S(1)}, bf16[128,896]{1,0:T(8,128)(2,1)}, u32[]{:S(2)}, u32[]{:S(2)}) collective-permute-start(bf16[128,896]{1,0:T(8,128)(2,1)S(1)} %bitcast.45), channel_id=1, source_target_pairs={{128,0},{132,4},{136,8},{140,12},{144,16},{148,20},{152,24},{156,2... | collective-permute-start | bytes 688136 | tf_op jit(solution)/shard_map/ppermute | solution.py:88
  182.6 15.8 %collective-permute-start.2 = (bf16[128,896]{1,0:T(8,128)(2,1)S(1)}, bf16[128,896]{1,0:T(8,128)(2,1)}, u32[]{:S(2)}, u32[]{:S(2)}) collective-permute-start(bf16[128,896]{1,0:T(8,128)(2,1)S(1)} %bitcast.46), channel_id=1, source_target_pairs={{120,0},{124,4},{0,8},{4,12},{8,16},{12,20},{16,24},{20,28},{24,32... | collective-permute-start | bytes 688136 | tf_op jit(solution)/shard_map/ppermute | solution.py:88
  186.5 10.3 %collective-permute-start.1 = (bf16[128,896]{1,0:T(8,128)(2,1)}, bf16[128,896]{1,0:T(8,128)(2,1)}, u32[]{:S(2)}, u32[]{:S(2)}) collective-permute-start(bf16[128,896]{1,0:T(8,128)(2,1)} %bitcast.47), channel_id=1, source_target_pairs={{8,0},{12,4},{16,8},{20,12},{24,16},{28,20},{32,24},{36,28},{40,32... | collective-permute-start | bytes 688136 | tf_op jit(solution)/shard_map/ppermute | solution.py:88
  192.9 9.7 %collective-permute-start.5 = (bf16[128,896]{1,0:T(8,128)(2,1)S(1)}, bf16[128,896]{1,0:T(8,128)(2,1)S(1)}, u32[]{:S(2)}, u32[]{:S(2)}) collective-permute-start(bf16[128,896]{1,0:T(8,128)(2,1)S(1)} %bitcast.48), channel_id=1, source_target_pairs={{12,0},{8,4},{20,8},{16,12},{28,16},{24,20},{36,24},{32,28},{44,32... | collective-permute-start | bytes 688136 | tf_op jit(solution)/shard_map/ppermute | solution.py:88
  315.5 1.7 copy-start.1
  318.2 21.2 %collective-permute-start.11 = (bf16[128,896]{1,0:T(8,128)(2,1)S(1)}, bf16[128,896]{1,0:T(8,128)(2,1)S(1)}, u32[]{:S(2)}, u32[]{:S(2)}) collective-permute-start(bf16[128,896]{1,0:T(8,128)(2,1)S(1)} %get-tuple-element.15), channel_id=1, source_target_pairs={{0,4},{4,0},{8,12},{12,8},{16,20},{20,16},{24,28},{28,24},{32,36},... | collective-permute-start | bytes 688136 | tf_op jit(solution)/shard_map/ppermute | solution.py:104
  325.3 22.8 %collective-permute-start.10 = (bf16[128,896]{1,0:T(8,128)(2,1)}, bf16[128,896]{1,0:T(8,128)(2,1)S(1)}, u32[]{:S(2)}, u32[]{:S(2)}) collective-permute-start(bf16[128,896]{1,0:T(8,128)(2,1)} %get-tuple-element.16), channel_id=1, source_target_pairs={{0,8},{4,12},{8,16},{12,20},{16,24},{20,28},{24,32},{28,36},{32,40... | collective-permute-start | bytes 688136 | tf_op jit(solution)/shard_map/ppermute | solution.py:104
  328.5 19.6 %collective-permute-start.9 = (bf16[128,896]{1,0:T(8,128)(2,1)}, bf16[128,896]{1,0:T(8,128)(2,1)S(1)}, u32[]{:S(2)}, u32[]{:S(2)}) collective-permute-start(bf16[128,896]{1,0:T(8,128)(2,1)} %get-tuple-element.17), channel_id=1, source_target_pairs={{0,120},{4,124},{8,0},{12,4},{16,8},{20,12},{24,16},{28,20},{32,24... | collective-permute-start | bytes 688136 | tf_op jit(solution)/shard_map/ppermute | solution.py:104
  332.9 15.2 %collective-permute-start.8 = (bf16[128,896]{1,0:T(8,128)(2,1)}, bf16[128,896]{1,0:T(8,128)(2,1)S(1)}, u32[]{:S(2)}, u32[]{:S(2)}) collective-permute-start(bf16[128,896]{1,0:T(8,128)(2,1)} %get-tuple-element.18), channel_id=1, source_target_pairs={{0,128},{4,132},{8,136},{12,140},{16,144},{20,148},{24,152},{28,15... | collective-permute-start | bytes 688136 | tf_op jit(solution)/shard_map/ppermute | solution.py:104
  336.0 12.1 %collective-permute-start.7 = (bf16[128,896]{1,0:T(8,128)(2,1)}, bf16[128,896]{1,0:T(8,128)(2,1)S(1)}, u32[]{:S(2)}, u32[]{:S(2)}) collective-permute-start(bf16[128,896]{1,0:T(8,128)(2,1)} %get-tuple-element.19), channel_id=1, source_target_pairs={{0,384},{4,388},{8,392},{12,396},{16,400},{20,404},{24,408},{28,41... | collective-permute-start | bytes 688136 | tf_op jit(solution)/shard_map/ppermute | solution.py:104
  339.4 11.1 %collective-permute-start.6 = (bf16[128,896]{1,0:T(8,128)(2,1)S(1)}, bf16[128,896]{1,0:T(8,128)(2,1)S(1)}, u32[]{:S(2)}, u32[]{:S(2)}) collective-permute-start(bf16[128,896]{1,0:T(8,128)(2,1)S(1)} %get-tuple-element.20), channel_id=1, source_target_pairs={{0,12},{4,8},{8,20},{12,16},{16,28},{20,24},{24,36},{28,32},{32,44... | collective-permute-start | bytes 688136 | tf_op jit(solution)/shard_map/ppermute | solution.py:104
  361.4 14.7 %copy-start.3 = (f32[128,8]{0,1:T(8,128)S(1)}, f32[128,8]{0,1:T(8,128)}, u32[]{:S(2)}) copy-start(f32[128,8]{0,1:T(8,128)} %param.7) | copy-start | bytes 12292
  361.4 124.5 %all-to-all-start.1 = ((bf16[128,8,1120]{2,1,0:T(8,128)(2,1)}), bf16[128,8,1120]{2,1,0:T(8,128)(2,1)}, u32[]{:S(2)}, u32[]{:S(2)}) async-start(bf16[128,8,1120]{2,1,0:T(8,128)(2,1)} %copy.79), calls=%async_computation.1 | async-start | bytes 4718592 | tf_op jit(solution)/shard_map/all_to_all | solution.py:29
Sparse Core Ops, SparseCore 0:
  211.3 96.9 all-reduce.2

commit v4 on v3

--- a/solution.py
+++ b/solution.py
@@ -30,10 +30,9 @@
     return moved_rows.reshape(shape)
 
 
-def silu_hidden(before):
-    summed = lax.psum(before.astype(jnp.bfloat16), "dp").astype(jnp.float32)
-    result = jax.nn.silu(summed).astype(jnp.bfloat16)
-    return result
+def silu_hidden(befores):
+    summed = lax.psum(tuple(b.astype(jnp.bfloat16) for b in befores), "dp")
+    return tuple(jax.nn.silu(v.astype(jnp.float32)).astype(jnp.bfloat16) for v in summed)
 
 
 def local(tokens, route_ids, gate_scores, up_weight, down_weight):
@@ -87,16 +86,15 @@
         pairs = [(int(moved(d, relays[i], experts, 1)), d) for d in range(experts)]
         hot_rows.append(lax.ppermute(outgoing, "expert", pairs))
 
-    flat_rows = jnp.concatenate(
-        [arrived[:, :cold_most].reshape(-1, features)] + hot_rows, axis=0
-    )
-    before = jnp.dot(flat_rows, up_local, preferred_element_type=jnp.float32)
-    hidden = silu_hidden(before)
-    output = jnp.dot(hidden, down_local, preferred_element_type=jnp.float32)
-    outcome = output.astype(jnp.bfloat16)
-    regular_count = experts * cold_most
-    regular_out = outcome[:regular_count].reshape(experts, cold_most, features)
-    hot_out = outcome[regular_count:].reshape(extra, experts, features)
+    regular_rows = arrived[:, :cold_most].reshape(-1, features)
+    hot_block = jnp.stack(hot_rows).reshape(-1, features)
+    regular_before = jnp.dot(regular_rows, up_local, preferred_element_type=jnp.float32)
+    hot_before = jnp.dot(hot_block, up_local, preferred_element_type=jnp.float32)
+    regular_hidden, hot_hidden = silu_hidden((regular_before, hot_before))
+    regular_out = jnp.dot(regular_hidden, down_local, preferred_element_type=jnp.float32)
+    hot_out = jnp.dot(hot_hidden, down_local, preferred_element_type=jnp.float32)
+    regular_out = regular_out.astype(jnp.bfloat16).reshape(experts, cold_most, features)
+    hot_out = hot_out.astype(jnp.bfloat16).reshape(extra, experts, features)
 
     back = []
     for i in range(1, extra):

time: 512 us -> 507 us (level)
  local copies, waits for them, and re-layouts: 71 us -> 61 us
    unnamed x16, local copies, waits for them, and re-layouts: 12.7 us -> 7 us
    dot_general x2 -> x4, matrix products: 15 us -> 19.9 us  [the longest x1 5.76 us: local(): jnp.dot(regular_hidden, down_local, preferred_element_type=jnp.float32)]
  transfers between devices with their start and end apart: 15 -> 15, of which waited for: 5 -> 4; matrix products, arithmetic and copies ran while one was open for 5% -> 5% of each run, Pallas kernels for 0% -> 0%
where the time goes in v4:
time: 507 us; the launch traced here: 506 us
  waiting for transfers between devices  315 us (62%)
  starting transfers between devices  74.2 us (15%)
  local copies, waits for them, and re-layouts  61 us (12%)
  between operations  23.4 us (5%)
  matrix products  19.9 us (4%)
  other arithmetic  12.5 us (2%)
    all_to_all x2, waiting for transfers between devices, exchange(): lax.all_to_all(packed, 'expert', split_axis=0, concat_axis=0, tiled=True)  214 us
    psum x1, waiting for transfers between devices, silu_hidden(): summed = lax.psum(tuple((b.astype(jnp.bfloat16) for b in befores)), 'dp')  99.7 us
    all_to_all x2, starting transfers between devices, exchange(): lax.all_to_all(packed, 'expert', split_axis=0, concat_axis=0, tiled=True)  37.7 us
    ppermute x6, starting transfers between devices, local(): back.append(lax.ppermute(hot_out[i], 'expert', pairs))  18.8 us
    ppermute x6, starting transfers between devices, local(): hot_rows.append(lax.ppermute(outgoing, 'expert', pairs))  17.7 us
    all_to_all x3, local copies, waits for them, and re-layouts, exchange(): lax.all_to_all(packed, 'expert', split_axis=0, concat_axis=0, tiled=True)  15 us
  transfers between devices with their start and end apart: 15, of which 4 were waited for; matrix products, arithmetic and copies ran while one was open for 5% of the time, Pallas kernels for 0%

profile of v4, /device:TPU:1, one launch (start us, length us, event | category | flops | bytes accessed | tf_op | source)
XLA Modules:
  0.0 505.6 jit_solution(12933422464622553981)
XLA Ops:
  8.5 2.5 top_k.11
  11.8 4.3 scatter_custom_fusion
  16.2 5.0 gather_fusion
  21.2 6.0 %all_to_all.12 = bf16[128,8,1120]{2,1,0:T(8,128)(2,1)} reshape(bf16[1280,896]{1,0:T(8,128)(2,1)} %gather_fusion) | data formatting | bytes 4587520 | tf_op jit(solution)/shard_map/all_to_all | solution.py:29
  27.2 20.8 %all-to-all-start = ((bf16[128,8,1120]{2,1,0:T(8,128)(2,1)}), bf16[128,8,1120]{2,1,0:T(8,128)(2,1)}, u32[]{:S(2)}, u32[]{:S(2)}) async-start(bf16[128,8,1120]{2,1,0:T(8,128)(2,1)} %all_to_all.12), calls=%async_computation | async-start | bytes 4718592 | tf_op jit(solution)/shard_map/all_to_all | solution.py:29
  53.5 104.3 %all-to-all-done = bf16[128,8,1120]{2,1,0:T(8,128)(2,1)} async-done(((bf16[128,8,1120]{2,1,0:T(8,128)(2,1)}), bf16[128,8,1120]{2,1,0:T(8,128)(2,1)}, u32[]{:S(2)}, u32[]{:S(2)}) %all-to-all-start) | async-done | bytes 2293792 | tf_op jit(solution)/shard_map/all_to_all | solution.py:29
  157.8 4.5 copy.56
  162.3 2.9 slice.105
  167.3 2.4 collective-permute-start
  169.8 2.3 collective-permute-start.1
  172.1 3.5 collective-permute-start.2
  175.6 3.3 collective-permute-start.3
  180.9 3.9 copy.57
  184.8 5.2 %convolution_convert_fusion = bf16[1024,1024]{1,0:T(8,128)(2,1)} fusion(bf16[1,896,1024]{2,1,0:T(8,128)(2,1)S(1)} %copy-done, bf16[128,8,896]{2,1,0:T(8,128)(2,1)} %copy.57), kind=kOutput, calls=%fused_computation.20 | convolution fusion | flops 1880096768 | bytes 5767168 | tf_op jit(solution)/shard_map/dot_general | solution.py:91
  191.1 4.2 collective-permute-start.5
  201.1 2.6 copy.60
  203.7 4.7 fusion.21
  208.5 99.7 %all-reduce.4.cloned.1.call-done = (bf16[896,1024]{1,0:T(8,128)(2,1)}, bf16[1024,1024]{1,0:T(8,128)(2,1)}) async-done(((bf16[896,1024]{1,0:T(8,128)(2,1)}, bf16[1024,1024]{1,0:T(8,128)(2,1)}), (bf16[896,1024]{1,0:T(8,128)(2,1)}, bf16[1024,1024]{1,0:T(8,128)(2,1)})) %all-reduce.4.cloned.1.call-update) | async-done | bytes 3932176 | tf_op jit(solution)/shard_map/psum | solution.py:34
  308.2 4.2 fusion.28
  313.6 3.2 collective-permute-start.10
  321.6 3.0 collective-permute-start.11
  324.6 3.1 collective-permute-start.6
  327.7 4.3 collective-permute-start.7
  334.0 3.3 collective-permute-start.9
  337.3 5.8 %convert_bitcast_fusion = bf16[128,8,896]{2,1,0:T(8,128)(2,1)} fusion(bf16[1,1024,896]{2,1,0:T(8,128)(2,1)} %param.9, bf16[1024,1024]{1,0:T(8,128)(2,1)} %get-tuple-element.14), kind=kOutput, calls=%fused_computation.29 | convolution fusion | flops 1886257152 | bytes 5767168 | tf_op jit(solution)/shard_map/dot_general | solution.py:94
  343.1 3.8 copy.61
  350.0 4.5 copy.62
  354.5 16.9 %all-to-all-start.1 = ((bf16[128,8,1120]{2,1,0:T(8,128)(2,1)}), bf16[128,8,1120]{2,1,0:T(8,128)(2,1)}, u32[]{:S(2)}, u32[]{:S(2)}) async-start(bf16[128,8,1120]{2,1,0:T(8,128)(2,1)} %copy.62), calls=%async_computation.1 | async-start | bytes 4718592 | tf_op jit(solution)/shard_map/all_to_all | solution.py:29
  371.5 109.6 %all-to-all-done.1 = bf16[128,8,1120]{2,1,0:T(8,128)(2,1)} async-done(((bf16[128,8,1120]{2,1,0:T(8,128)(2,1)}), bf16[128,8,1120]{2,1,0:T(8,128)(2,1)}, u32[]{:S(2)}, u32[]{:S(2)}) %all-to-all-start.1) | async-done | bytes 2293792 | tf_op jit(solution)/shard_map/all_to_all | solution.py:29
  481.2 6.5 %reshape_reshape.7 = bf16[1280,896]{1,0:T(8,128)(2,1)} reshape(bf16[128,8,1120]{2,1,0:T(8,128)(2,1)} %all-to-all-done.1) | data formatting | bytes 4587520 | tf_op jit(solution)/shard_map/reshape;reshape | solution.py:112
  487.7 7.7 %gather_fusion.1 = bf16[1024,896]{1,0:T(8,128)(2,1)} fusion(bf16[1280,896]{1,0:T(8,128)(2,1)} %reshape_reshape.7, s32[1024]{0:T(1024)S(1)} %get-tuple-element.15), kind=kCustom, calls=%fused_computation.1 | custom fusion | bytes 3674112 | tf_op jit(solution)/shard_map/gather | solution.py:112
  495.3 3.4 fusion.8
  (61 shorter events, 20.9 us)
Async XLA Ops:
  6.5 178.3 %copy-start = (bf16[1,896,1024]{2,1,0:T(8,128)(2,1)S(1)}, bf16[1,896,1024]{2,1,0:T(8,128)(2,1)}, u32[]{:S(2)}) copy-start(bf16[1,896,1024]{2,1,0:T(8,128)(2,1)} %param.8) | copy-start | bytes 5505028
  6.5 9.6 %copy-start.2 = (bf16[128,896]{1,0:T(8,128)(2,1)S(1)}, bf16[128,896]{1,0:T(8,128)(2,1)}, u32[]{:S(2)}) copy-start(bf16[128,896]{1,0:T(8,128)(2,1)} %param.5) | copy-start | bytes 688132
  27.2 130.6 %all-to-all-start = ((bf16[128,8,1120]{2,1,0:T(8,128)(2,1)}), bf16[128,8,1120]{2,1,0:T(8,128)(2,1)}, u32[]{:S(2)}, u32[]{:S(2)}) async-start(bf16[128,8,1120]{2,1,0:T(8,128)(2,1)} %all_to_all.12), calls=%async_computation | async-start | bytes 4718592 | tf_op jit(solution)/shard_map/all_to_all | solution.py:29
  48.0 260.2 %all-reduce.4.cloned.1.call-start = ((), (), s32[]{:S(2)}) async-start(), calls=%async_computation.2 | async-start | bytes 7864320 | tf_op jit(solution)/shard_map/psum | solution.py:34
  167.3 23.8 %collective-permute-start = (bf16[128,896]{0,1:T(8,128)(2,1)}, bf16[128,896]{0,1:T(8,128)(2,1)}, u32[]{:S(2)}, u32[]{:S(2)}) collective-permute-start(bf16[128,896]{0,1:T(8,128)(2,1)} %get-tuple-element.22), channel_id=1, source_target_pairs={{4,0},{0,4},{12,8},{8,12},{20,16},{16,20},{28,24},{24,28},{36,32},... | collective-permute-start | bytes 688136 | tf_op jit(solution)/shard_map/ppermute | solution.py:87
  169.8 26.5 %collective-permute-start.1 = (bf16[128,896]{0,1:T(8,128)(2,1)}, bf16[128,896]{0,1:T(8,128)(2,1)}, u32[]{:S(2)}, u32[]{:S(2)}) collective-permute-start(bf16[128,896]{0,1:T(8,128)(2,1)} %get-tuple-element.18), channel_id=1, source_target_pairs={{8,0},{12,4},{16,8},{20,12},{24,16},{28,20},{32,24},{36,28},{40,32... | collective-permute-start | bytes 688136 | tf_op jit(solution)/shard_map/ppermute | solution.py:87
  172.1 25.2 %collective-permute-start.2 = (bf16[128,896]{0,1:T(8,128)(2,1)}, bf16[128,896]{0,1:T(8,128)(2,1)}, u32[]{:S(2)}, u32[]{:S(2)}) collective-permute-start(bf16[128,896]{0,1:T(8,128)(2,1)} %get-tuple-element.19), channel_id=1, source_target_pairs={{120,0},{124,4},{0,8},{4,12},{8,16},{12,20},{16,24},{20,28},{24,32... | collective-permute-start | bytes 688136 | tf_op jit(solution)/shard_map/ppermute | solution.py:87
  175.6 22.6 %collective-permute-start.3 = (bf16[128,896]{0,1:T(8,128)(2,1)}, bf16[128,896]{0,1:T(8,128)(2,1)}, u32[]{:S(2)}, u32[]{:S(2)}) collective-permute-start(bf16[128,896]{0,1:T(8,128)(2,1)} %get-tuple-element.20), channel_id=1, source_target_pairs={{128,0},{132,4},{136,8},{140,12},{144,16},{148,20},{152,24},{156,2... | collective-permute-start | bytes 688136 | tf_op jit(solution)/shard_map/ppermute | solution.py:87
  178.9 20.3 %collective-permute-start.4 = (bf16[128,896]{0,1:T(8,128)(2,1)}, bf16[128,896]{0,1:T(8,128)(2,1)}, u32[]{:S(2)}, u32[]{:S(2)}) collective-permute-start(bf16[128,896]{0,1:T(8,128)(2,1)} %get-tuple-element.21), channel_id=1, source_target_pairs={{384,0},{388,4},{392,8},{396,12},{400,16},{404,20},{408,24},{412,2... | collective-permute-start | bytes 688136 | tf_op jit(solution)/shard_map/ppermute | solution.py:87
  184.8 6.3 %copy-start.3 = (bf16[128,896]{0,1:T(8,128)(2,1)S(1)}, bf16[128,896]{0,1:T(8,128)(2,1)}, u32[]{:S(2)}) copy-start(bf16[128,896]{0,1:T(8,128)(2,1)} %get-tuple-element.17) | copy-start | bytes 688132
  191.1 10.0 %collective-permute-start.5 = (bf16[128,896]{0,1:T(8,128)(2,1)S(1)}, bf16[128,896]{0,1:T(8,128)(2,1)S(1)}, u32[]{:S(2)}, u32[]{:S(2)}) collective-permute-start(bf16[128,896]{0,1:T(8,128)(2,1)S(1)} %copy-done.3), channel_id=1, source_target_pairs={{12,0},{8,4},{20,8},{16,12},{28,16},{24,20},{36,24},{32,28},{44,32... | collective-permute-start | bytes 688136 | tf_op jit(solution)/shard_map/ppermute | solution.py:87
  313.6 20.4 %collective-permute-start.10 = (bf16[128,896]{0,1:T(8,128)(2,1)}, bf16[128,896]{0,1:T(8,128)(2,1)}, u32[]{:S(2)}, u32[]{:S(2)}) collective-permute-start(bf16[128,896]{0,1:T(8,128)(2,1)} %get-tuple-element.24), channel_id=1, source_target_pairs={{0,8},{4,12},{8,16},{12,20},{16,24},{20,28},{24,32},{28,36},{32,40... | collective-permute-start | bytes 688136 | tf_op jit(solution)/shard_map/ppermute | solution.py:102
  321.6 25.3 %collective-permute-start.11 = (bf16[128,896]{0,1:T(8,128)(2,1)}, bf16[128,896]{0,1:T(8,128)(2,1)}, u32[]{:S(2)}, u32[]{:S(2)}) collective-permute-start(bf16[128,896]{0,1:T(8,128)(2,1)} %get-tuple-element.23), channel_id=1, source_target_pairs={{0,4},{4,0},{8,12},{12,8},{16,20},{20,16},{24,28},{28,24},{32,36},... | collective-permute-start | bytes 688136 | tf_op jit(solution)/shard_map/ppermute | solution.py:102
  324.6 22.2 %collective-permute-start.6 = (bf16[128,896]{0,1:T(8,128)(2,1)}, bf16[128,896]{0,1:T(8,128)(2,1)}, u32[]{:S(2)}, u32[]{:S(2)}) collective-permute-start(bf16[128,896]{0,1:T(8,128)(2,1)} %get-tuple-element.28), channel_id=1, source_target_pairs={{0,12},{4,8},{8,20},{12,16},{16,28},{20,24},{24,36},{28,32},{32,44... | collective-permute-start | bytes 688136 | tf_op jit(solution)/shard_map/ppermute | solution.py:102
  327.7 19.2 %collective-permute-start.7 = (bf16[128,896]{0,1:T(8,128)(2,1)}, bf16[128,896]{0,1:T(8,128)(2,1)}, u32[]{:S(2)}, u32[]{:S(2)}) collective-permute-start(bf16[128,896]{0,1:T(8,128)(2,1)} %get-tuple-element.27), channel_id=1, source_target_pairs={{0,384},{4,388},{8,392},{12,396},{16,400},{20,404},{24,408},{28,41... | collective-permute-start | bytes 688136 | tf_op jit(solution)/shard_map/ppermute | solution.py:102
  332.0 14.8 %collective-permute-start.8 = (bf16[128,896]{0,1:T(8,128)(2,1)}, bf16[128,896]{0,1:T(8,128)(2,1)}, u32[]{:S(2)}, u32[]{:S(2)}) collective-permute-start(bf16[128,896]{0,1:T(8,128)(2,1)} %get-tuple-element.26), channel_id=1, source_target_pairs={{0,128},{4,132},{8,136},{12,140},{16,144},{20,148},{24,152},{28,15... | collective-permute-start | bytes 688136 | tf_op jit(solution)/shard_map/ppermute | solution.py:102
  334.0 12.9 %collective-permute-start.9 = (bf16[128,896]{0,1:T(8,128)(2,1)}, bf16[128,896]{0,1:T(8,128)(2,1)}, u32[]{:S(2)}, u32[]{:S(2)}) collective-permute-start(bf16[128,896]{0,1:T(8,128)(2,1)} %get-tuple-element.25), channel_id=1, source_target_pairs={{0,120},{4,124},{8,0},{12,4},{16,8},{20,12},{24,16},{28,20},{32,24... | collective-permute-start | bytes 688136 | tf_op jit(solution)/shard_map/ppermute | solution.py:102
  346.9 1.5 copy-start.1
  354.5 16.9 %copy-start.4 = (f32[128,8]{0,1:T(8,128)S(1)}, f32[128,8]{0,1:T(8,128)}, u32[]{:S(2)}) copy-start(f32[128,8]{0,1:T(8,128)} %param.7) | copy-start | bytes 12292
  354.5 126.7 %all-to-all-start.1 = ((bf16[128,8,1120]{2,1,0:T(8,128)(2,1)}), bf16[128,8,1120]{2,1,0:T(8,128)(2,1)}, u32[]{:S(2)}, u32[]{:S(2)}) async-start(bf16[128,8,1120]{2,1,0:T(8,128)(2,1)} %copy.62), calls=%async_computation.1 | async-start | bytes 4718592 | tf_op jit(solution)/shard_map/all_to_all | solution.py:29
Sparse Core Ops, SparseCore 0:
  208.6 99.5 all-reduce.3

commit v5 on v4

--- a/solution.py
+++ b/solution.py
@@ -31,8 +31,22 @@
 
 
 def silu_hidden(befores):
-    summed = lax.psum(tuple(b.astype(jnp.bfloat16) for b in befores), "dp")
-    return tuple(jax.nn.silu(v.astype(jnp.float32)).astype(jnp.bfloat16) for v in summed)
+    peers = lax.axis_size("dp")
+    widths = [b.shape[0] // peers for b in befores]
+    blocks = jnp.concatenate(
+        [b.astype(jnp.bfloat16).reshape(peers, w, b.shape[1]) for b, w in zip(befores, widths)], axis=1
+    )
+    parts = lax.all_to_all(blocks, "dp", 0, 0, tiled=True)
+    summed = jnp.sum(parts.astype(jnp.float32), axis=0)
+    hidden = jax.nn.silu(summed).astype(jnp.bfloat16)
+    spread = jnp.broadcast_to(hidden[None], (peers,) + hidden.shape)
+    gathered = lax.all_to_all(spread, "dp", 0, 0, tiled=True)
+    results = []
+    start = 0
+    for b, w in zip(befores, widths):
+        results.append(gathered[:, start:start + w].reshape(b.shape))
+        start += w
+    return tuple(results)
 
 
 def local(tokens, route_ids, gate_scores, up_weight, down_weight):

time: 507 us -> 485 us (0.957)
  waiting for transfers between devices: 315 us -> 215 us
  blocking collectives: 0 us -> 97.1 us
  between operations: 23.4 us -> 10.1 us
  starting transfers between devices: 74.2 us -> 68.5 us
  matrix products: 19.9 us -> 14.6 us
    psum x1 -> x0, waiting for transfers between devices: 99.7 us -> none  [silu_hidden(): summed = lax.psum(tuple((b.astype(jnp.bfloat16) for b in befores)), 'dp')]
    all_to_all x0 -> x2, blocking collectives: none -> 97.1 us  [the longest x1 49.7 us: silu_hidden(): parts = lax.all_to_all(blocks, 'dp', 0, 0, tiled=True)]
    all_to_all x2, starting transfers between devices: 37.7 us -> 31.3 us  [exchange(): lax.all_to_all(packed, 'expert', split_axis=0, concat_axis=0, tiled=True)]
  transfers between devices with their start and end apart: 15 -> 14, of which waited for: 4 -> 4; matrix products, arithmetic and copies ran while one was open for 5% -> 5% of each run, Pallas kernels for 0% -> 0%
where the time goes in v5:
time: 485 us; the launch traced here: 484 us
  waiting for transfers between devices  215 us (44%)
  blocking collectives  97.1 us (20%)
  starting transfers between devices  68.5 us (14%)
  local copies, waits for them, and re-layouts  63.2 us (13%)
  other arithmetic  15.2 us (3%)
  matrix products  14.6 us (3%)
  between operations  10.1 us (2%)
    all_to_all x2, waiting for transfers between devices, exchange(): lax.all_to_all(packed, 'expert', split_axis=0, concat_axis=0, tiled=True)  214 us
    all_to_all x1, blocking collectives, silu_hidden(): parts = lax.all_to_all(blocks, 'dp', 0, 0, tiled=True)  49.7 us
    all_to_all x1, blocking collectives, silu_hidden(): gathered = lax.all_to_all(spread, 'dp', 0, 0, tiled=True)  47.4 us
    all_to_all x2, starting transfers between devices, exchange(): lax.all_to_all(packed, 'expert', split_axis=0, concat_axis=0, tiled=True)  31.3 us
    ppermute x6, starting transfers between devices, local(): back.append(lax.ppermute(hot_out[i], 'expert', pairs))  19.7 us
    ppermute x6, starting transfers between devices, local(): hot_rows.append(lax.ppermute(outgoing, 'expert', pairs))  17.5 us
    all_to_all x3, local copies, waits for them, and re-layouts, exchange(): lax.all_to_all(packed, 'expert', split_axis=0, concat_axis=0, tiled=True)  15 us
  transfers between devices with their start and end apart: 14, of which 4 were waited for; matrix products, arithmetic and copies ran while one was open for 5% of the time, Pallas kernels for 0%

profile of v5, /device:TPU:1, one launch (start us, length us, event | category | flops | bytes accessed | tf_op | source)
XLA Modules:
  0.0 483.8 jit_solution(17314560147066565232)
XLA Ops:
  2.0 2.5 top_k.11
  5.3 4.3 scatter_custom_fusion
  9.7 5.0 %gather_fusion = bf16[1280,896]{1,0:T(8,128)(2,1)} fusion(bf16[129,896]{1,0:T(8,128)(2,1)S(1)} %concatenate.9, s32[2048]{0:T(1024)S(1)} %pad_clamp_fusion), kind=kCustom, calls=%fused_computation | custom fusion | bytes 4592640 | tf_op jit(solution)/shard_map/gather | solution.py:91
  14.6 6.0 %all_to_all.18 = bf16[128,8,1120]{2,1,0:T(8,128)(2,1)} reshape(bf16[1280,896]{1,0:T(8,128)(2,1)} %gather_fusion) | data formatting | bytes 4587520 | tf_op jit(solution)/shard_map/all_to_all | solution.py:29
  20.7 20.8 %all-to-all-start = ((bf16[128,8,1120]{2,1,0:T(8,128)(2,1)}), bf16[128,8,1120]{2,1,0:T(8,128)(2,1)}, u32[]{:S(2)}, u32[]{:S(2)}) async-start(bf16[128,8,1120]{2,1,0:T(8,128)(2,1)} %all_to_all.18), calls=%async_computation | async-start | bytes 4718592 | tf_op jit(solution)/shard_map/all_to_all | solution.py:29
  46.9 104.3 %all-to-all-done = bf16[128,8,1120]{2,1,0:T(8,128)(2,1)} async-done(((bf16[128,8,1120]{2,1,0:T(8,128)(2,1)}), bf16[128,8,1120]{2,1,0:T(8,128)(2,1)}, u32[]{:S(2)}, u32[]{:S(2)}) %all-to-all-start) | async-done | bytes 2293792 | tf_op jit(solution)/shard_map/all_to_all | solution.py:29
  151.3 4.5 copy.56
  155.8 2.9 slice.113
  158.6 2.2 select_bitcast_fusion.2
  160.8 2.4 collective-permute-start
  163.3 2.3 collective-permute-start.1
  165.6 3.5 collective-permute-start.2
  169.1 3.3 collective-permute-start.3
  174.4 3.9 copy.57
  178.3 5.2 %convolution_convert_fusion = bf16[1024,1024]{1,0:T(8,128)(2,1)} fusion(bf16[1,896,1024]{2,1,0:T(8,128)(2,1)S(1)} %copy-done, bf16[128,8,896]{2,1,0:T(8,128)(2,1)} %copy.57), kind=kOutput, calls=%fused_computation.9 | convolution fusion | flops 1880096768 | bytes 5767168 | tf_op jit(solution)/shard_map/dot_general | solution.py:105
  184.7 4.0 collective-permute-start.5
  194.7 2.6 copy.60
  197.3 3.6 fusion.9
  201.3 49.7 %all_to_all.28 = bf16[4,480,1024]{2,1,0:T(8,128)(2,1)S(1)} all-to-all(bf16[4,480,1024]{2,1,0:T(8,128)(2,1)S(1)} %pad_maximum_fusion), channel_id=1, replica_groups=mesh['expert'=128,'dp'=4] {'dp'}, dimensions={0} | all-to-all | bytes 7864320 | tf_op jit(solution)/shard_map/all_to_all | solution.py:39
  252.9 47.4 %all_to_all.29 = bf16[4,480,1024]{2,1,0:T(8,128)(2,1)S(1)} all-to-all(bf16[4,480,1024]{2,1,0:T(8,128)(2,1)S(1)} %broadcast_in_dim.30), channel_id=1, replica_groups=mesh['expert'=128,'dp'=4] {'dp'}, dimensions={0} | all-to-all | bytes 7864320 | tf_op jit(solution)/shard_map/all_to_all | solution.py:43
  313.7 4.7 collective-permute-start.11
  318.4 3.8 collective-permute-start.6
  322.2 5.1 %collective-permute-start.7 = (bf16[128,896]{0,1:T(8,128)(2,1)}, bf16[128,896]{0,1:T(8,128)(2,1)}, u32[]{:S(2)}, u32[]{:S(2)}) collective-permute-start(bf16[128,896]{0,1:T(8,128)(2,1)} %get-tuple-element.25), channel_id=1, source_target_pairs={{0,384},{4,388},{8,392},{12,396},{16,400},{20,404},{24,408},{28,41... | collective-permute-start | bytes 688136 | tf_op jit(solution)/shard_map/ppermute | solution.py:116
  327.3 2.2 collective-permute-start.8
  331.6 3.6 convert_bitcast_fusion
  335.2 3.1 copy.61
  341.3 4.5 copy.62
  345.8 10.5 %all-to-all-start.3 = ((bf16[128,8,1120]{2,1,0:T(8,128)(2,1)}), bf16[128,8,1120]{2,1,0:T(8,128)(2,1)}, u32[]{:S(2)}, u32[]{:S(2)}) async-start(bf16[128,8,1120]{2,1,0:T(8,128)(2,1)} %copy.62), calls=%async_computation.3 | async-start | bytes 4718592 | tf_op jit(solution)/shard_map/all_to_all | solution.py:29
  356.5 109.6 %all-to-all-done.3 = bf16[128,8,1120]{2,1,0:T(8,128)(2,1)} async-done(((bf16[128,8,1120]{2,1,0:T(8,128)(2,1)}), bf16[128,8,1120]{2,1,0:T(8,128)(2,1)}, u32[]{:S(2)}, u32[]{:S(2)}) %all-to-all-start.3) | async-done | bytes 2293792 | tf_op jit(solution)/shard_map/all_to_all | solution.py:29
  466.1 6.5 %reshape_reshape.7 = bf16[1280,896]{1,0:T(8,128)(2,1)} reshape(bf16[128,8,1120]{2,1,0:T(8,128)(2,1)} %all-to-all-done.3) | data formatting | bytes 4587520 | tf_op jit(solution)/shard_map/reshape;reshape | solution.py:126
  472.6 7.8 %gather_fusion.1 = bf16[1024,896]{1,0:T(8,128)(2,1)} fusion(bf16[1280,896]{1,0:T(8,128)(2,1)} %reshape_reshape.7, s32[1024]{0:T(1024)S(1)} %get-tuple-element.13), kind=kCustom, calls=%fused_computation.1 | custom fusion | bytes 3674112 | tf_op jit(solution)/shard_map/gather | solution.py:126
  480.4 3.4 fusion
  (79 shorter events, 28.4 us)
Async XLA Ops:
  0.0 178.3 %copy-start = (bf16[1,896,1024]{2,1,0:T(8,128)(2,1)S(1)}, bf16[1,896,1024]{2,1,0:T(8,128)(2,1)}, u32[]{:S(2)}) copy-start(bf16[1,896,1024]{2,1,0:T(8,128)(2,1)} %param.8) | copy-start | bytes 5505028
  0.0 9.6 %copy-start.6 = (bf16[128,896]{1,0:T(8,128)(2,1)S(1)}, bf16[128,896]{1,0:T(8,128)(2,1)}, u32[]{:S(2)}) copy-start(bf16[128,896]{1,0:T(8,128)(2,1)} %param.5) | copy-start | bytes 688132
  20.7 130.6 %all-to-all-start = ((bf16[128,8,1120]{2,1,0:T(8,128)(2,1)}), bf16[128,8,1120]{2,1,0:T(8,128)(2,1)}, u32[]{:S(2)}, u32[]{:S(2)}) async-start(bf16[128,8,1120]{2,1,0:T(8,128)(2,1)} %all_to_all.18), calls=%async_computation | async-start | bytes 4718592 | tf_op jit(solution)/shard_map/all_to_all | solution.py:29
  160.8 23.8 %collective-permute-start = (bf16[128,896]{0,1:T(8,128)(2,1)}, bf16[128,896]{0,1:T(8,128)(2,1)}, u32[]{:S(2)}, u32[]{:S(2)}) collective-permute-start(bf16[128,896]{0,1:T(8,128)(2,1)} %get-tuple-element.20), channel_id=1, source_target_pairs={{4,0},{0,4},{12,8},{8,12},{20,16},{16,20},{28,24},{24,28},{36,32},... | collective-permute-start | bytes 688136 | tf_op jit(solution)/shard_map/ppermute | solution.py:101
  163.3 26.4 %collective-permute-start.1 = (bf16[128,896]{0,1:T(8,128)(2,1)}, bf16[128,896]{0,1:T(8,128)(2,1)}, u32[]{:S(2)}, u32[]{:S(2)}) collective-permute-start(bf16[128,896]{0,1:T(8,128)(2,1)} %get-tuple-element.16), channel_id=1, source_target_pairs={{8,0},{12,4},{16,8},{20,12},{24,16},{28,20},{32,24},{36,28},{40,32... | collective-permute-start | bytes 688136 | tf_op jit(solution)/shard_map/ppermute | solution.py:101
  165.6 25.1 %collective-permute-start.2 = (bf16[128,896]{0,1:T(8,128)(2,1)}, bf16[128,896]{0,1:T(8,128)(2,1)}, u32[]{:S(2)}, u32[]{:S(2)}) collective-permute-start(bf16[128,896]{0,1:T(8,128)(2,1)} %get-tuple-element.17), channel_id=1, source_target_pairs={{120,0},{124,4},{0,8},{4,12},{8,16},{12,20},{16,24},{20,28},{24,32... | collective-permute-start | bytes 688136 | tf_op jit(solution)/shard_map/ppermute | solution.py:101
  169.1 22.5 %collective-permute-start.3 = (bf16[128,896]{0,1:T(8,128)(2,1)}, bf16[128,896]{0,1:T(8,128)(2,1)}, u32[]{:S(2)}, u32[]{:S(2)}) collective-permute-start(bf16[128,896]{0,1:T(8,128)(2,1)} %get-tuple-element.18), channel_id=1, source_target_pairs={{128,0},{132,4},{136,8},{140,12},{144,16},{148,20},{152,24},{156,2... | collective-permute-start | bytes 688136 | tf_op jit(solution)/shard_map/ppermute | solution.py:101
  172.4 20.2 %collective-permute-start.4 = (bf16[128,896]{0,1:T(8,128)(2,1)}, bf16[128,896]{0,1:T(8,128)(2,1)}, u32[]{:S(2)}, u32[]{:S(2)}) collective-permute-start(bf16[128,896]{0,1:T(8,128)(2,1)} %get-tuple-element.19), channel_id=1, source_target_pairs={{384,0},{388,4},{392,8},{396,12},{400,16},{404,20},{408,24},{412,2... | collective-permute-start | bytes 688136 | tf_op jit(solution)/shard_map/ppermute | solution.py:101
  178.3 6.3 %copy-start.7 = (bf16[128,896]{0,1:T(8,128)(2,1)S(1)}, bf16[128,896]{0,1:T(8,128)(2,1)}, u32[]{:S(2)}) copy-start(bf16[128,896]{0,1:T(8,128)(2,1)} %get-tuple-element.15) | copy-start | bytes 688132
  184.7 10.0 %collective-permute-start.5 = (bf16[128,896]{0,1:T(8,128)(2,1)S(1)}, bf16[128,896]{0,1:T(8,128)(2,1)S(1)}, u32[]{:S(2)}, u32[]{:S(2)}) collective-permute-start(bf16[128,896]{0,1:T(8,128)(2,1)S(1)} %copy-done.7), channel_id=1, source_target_pairs={{12,0},{8,4},{20,8},{16,12},{28,16},{24,20},{36,24},{32,28},{44,32... | collective-permute-start | bytes 688136 | tf_op jit(solution)/shard_map/ppermute | solution.py:101
  197.3 3.6 copy-start.3
  300.3 1.9 copy-start.2
  302.2 1.5 copy-start.9
  307.0 22.6 %collective-permute-start.10 = (bf16[128,896]{0,1:T(8,128)(2,1)S(1)}, bf16[128,896]{0,1:T(8,128)(2,1)S(1)}, u32[]{:S(2)}, u32[]{:S(2)}) collective-permute-start(bf16[128,896]{0,1:T(8,128)(2,1)S(1)} %get-tuple-element.22), channel_id=1, source_target_pairs={{0,8},{4,12},{8,16},{12,20},{16,24},{20,28},{24,32},{28,36},{32,40... | collective-permute-start | bytes 688136 | tf_op jit(solution)/shard_map/ppermute | solution.py:116
  313.7 24.6 %collective-permute-start.11 = (bf16[128,896]{0,1:T(8,128)(2,1)}, bf16[128,896]{0,1:T(8,128)(2,1)}, u32[]{:S(2)}, u32[]{:S(2)}) collective-permute-start(bf16[128,896]{0,1:T(8,128)(2,1)} %get-tuple-element.21), channel_id=1, source_target_pairs={{0,4},{4,0},{8,12},{12,8},{16,20},{20,16},{24,28},{28,24},{32,36},... | collective-permute-start | bytes 688136 | tf_op jit(solution)/shard_map/ppermute | solution.py:116
  318.4 19.9 %collective-permute-start.6 = (bf16[128,896]{0,1:T(8,128)(2,1)}, bf16[128,896]{0,1:T(8,128)(2,1)}, u32[]{:S(2)}, u32[]{:S(2)}) collective-permute-start(bf16[128,896]{0,1:T(8,128)(2,1)} %get-tuple-element.26), channel_id=1, source_target_pairs={{0,12},{4,8},{8,20},{12,16},{16,28},{20,24},{24,36},{28,32},{32,44... | collective-permute-start | bytes 688136 | tf_op jit(solution)/shard_map/ppermute | solution.py:116
  322.2 16.2 %collective-permute-start.7 = (bf16[128,896]{0,1:T(8,128)(2,1)}, bf16[128,896]{0,1:T(8,128)(2,1)}, u32[]{:S(2)}, u32[]{:S(2)}) collective-permute-start(bf16[128,896]{0,1:T(8,128)(2,1)} %get-tuple-element.25), channel_id=1, source_target_pairs={{0,384},{4,388},{8,392},{12,396},{16,400},{20,404},{24,408},{28,41... | collective-permute-start | bytes 688136 | tf_op jit(solution)/shard_map/ppermute | solution.py:116
  327.3 4.2 slice-start
  327.3 4.2 copy-start.10
  327.3 11.0 %collective-permute-start.8 = (bf16[128,896]{0,1:T(8,128)(2,1)}, bf16[128,896]{0,1:T(8,128)(2,1)}, u32[]{:S(2)}, u32[]{:S(2)}) collective-permute-start(bf16[128,896]{0,1:T(8,128)(2,1)} %get-tuple-element.24), channel_id=1, source_target_pairs={{0,128},{4,132},{8,136},{12,140},{16,144},{20,148},{24,152},{28,15... | collective-permute-start | bytes 688136 | tf_op jit(solution)/shard_map/ppermute | solution.py:116
  329.6 2.0 copy-start.4
  329.6 8.9 %collective-permute-start.9 = (bf16[128,896]{0,1:T(8,128)(2,1)}, bf16[128,896]{0,1:T(8,128)(2,1)}, u32[]{:S(2)}, u32[]{:S(2)}) collective-permute-start(bf16[128,896]{0,1:T(8,128)(2,1)} %get-tuple-element.23), channel_id=1, source_target_pairs={{0,120},{4,124},{8,0},{12,4},{16,8},{20,12},{24,16},{28,20},{32,24... | collective-permute-start | bytes 688136 | tf_op jit(solution)/shard_map/ppermute | solution.py:116
  338.3 1.2 copy-start.5
  345.8 10.5 %copy-start.8 = (f32[128,8]{0,1:T(8,128)S(1)}, f32[128,8]{0,1:T(8,128)}, u32[]{:S(2)}) copy-start(f32[128,8]{0,1:T(8,128)} %param.7) | copy-start | bytes 12292
  345.8 120.3 %all-to-all-start.3 = ((bf16[128,8,1120]{2,1,0:T(8,128)(2,1)}), bf16[128,8,1120]{2,1,0:T(8,128)(2,1)}, u32[]{:S(2)}, u32[]{:S(2)}) async-start(bf16[128,8,1120]{2,1,0:T(8,128)(2,1)} %copy.62), calls=%async_computation.3 | async-start | bytes 4718592 | tf_op jit(solution)/shard_map/all_to_all | solution.py:29
  472.6 11.2 %copy-start.1 = (bf16[1,896,1024]{2,1,0:T(8,128)(2,1)S(1)}, bf16[1,896,1024]{2,1,0:T(8,128)(2,1)}, u32[]{:S(2)}) copy-start(bf16[1,896,1024]{2,1,0:T(8,128)(2,1)} %param.8) | copy-start | bytes 5505028

commit v6 on v5

--- a/solution.py
+++ b/solution.py
@@ -123,9 +123,15 @@
         relay_out.append(result[:, None])
     outgoing = jnp.concatenate([regular_out] + relay_out, axis=1)
     returned = exchange(outgoing, experts)
-    picked = returned.reshape(-1, features)[position]
-    picked = picked.reshape(token_count, chosen_count, features).astype(jnp.float32)
-    mixed = jnp.sum(mix_weights[:, :, None] * picked, axis=1)
+    slot_range = jnp.arange(experts * slots, dtype=jnp.int32)
+    chosen_at = position.reshape(token_count, chosen_count)[:, :, None] == slot_range[None, None, :]
+    mixing = jnp.sum(jnp.where(chosen_at, mix_weights[:, :, None], 0.0), axis=1)
+    mixed = jnp.dot(
+        mixing,
+        returned.reshape(-1, features).astype(jnp.float32),
+        precision=lax.Precision.HIGHEST,
+        preferred_element_type=jnp.float32,
+    )
     return mixed.astype(jnp.bfloat16)
 
 

time: 485 us -> 478 us (0.986)
  local copies, waits for them, and re-layouts: 63.2 us -> 56.2 us
    gather x1 -> x0, local copies, waits for them, and re-layouts: 7.81 us -> none  [local(): picked = returned.reshape(-1, features)[position]]
where the time goes in v6:
time: 478 us; the launch traced here: 476 us
  waiting for transfers between devices  213 us (45%)
  blocking collectives  97.1 us (20%)
  starting transfers between devices  68.8 us (14%)
  local copies, waits for them, and re-layouts  56.2 us (12%)
  matrix products  18.1 us (4%)
  other arithmetic  12.5 us (3%)
  between operations  10.1 us (2%)
    all_to_all x2, waiting for transfers between devices, exchange(): lax.all_to_all(packed, 'expert', split_axis=0, concat_axis=0, tiled=True)  212 us
    all_to_all x1, blocking collectives, silu_hidden(): parts = lax.all_to_all(blocks, 'dp', 0, 0, tiled=True)  49.7 us
    all_to_all x1, blocking collectives, silu_hidden(): gathered = lax.all_to_all(spread, 'dp', 0, 0, tiled=True)  47.4 us
    all_to_all x2, starting transfers between devices, exchange(): lax.all_to_all(packed, 'expert', split_axis=0, concat_axis=0, tiled=True)  31.6 us
    ppermute x6, starting transfers between devices, local(): back.append(lax.ppermute(hot_out[i], 'expert', pairs))  19.7 us
    ppermute x6, starting transfers between devices, local(): hot_rows.append(lax.ppermute(outgoing, 'expert', pairs))  17.5 us
    all_to_all x3, local copies, waits for them, and re-layouts, exchange(): lax.all_to_all(packed, 'expert', split_axis=0, concat_axis=0, tiled=True)  15 us
    unnamed x28, local copies, waits for them, and re-layouts  9.77 us
  transfers between devices with their start and end apart: 14, of which 4 were waited for; matrix products, arithmetic and copies ran while one was open for 5% of the time, Pallas kernels for 0%

profile of v6, /device:TPU:1, one launch (start us, length us, event | category | flops | bytes accessed | tf_op | source)
XLA Modules:
  0.0 476.3 jit_solution(6209278960560035757)
XLA Ops:
  2.0 2.5 top_k.11
  5.3 4.3 scatter_custom_fusion
  9.7 5.0 %gather_fusion = bf16[1280,896]{1,0:T(8,128)(2,1)} fusion(bf16[129,896]{1,0:T(8,128)(2,1)S(1)} %concatenate.9, s32[2048]{0:T(1024)S(1)} %pad_clamp_fusion), kind=kCustom, calls=%fused_computation | custom fusion | bytes 4592640 | tf_op jit(solution)/shard_map/gather | solution.py:91
  14.6 6.0 %all_to_all.18 = bf16[128,8,1120]{2,1,0:T(8,128)(2,1)} reshape(bf16[1280,896]{1,0:T(8,128)(2,1)} %gather_fusion) | data formatting | bytes 4587520 | tf_op jit(solution)/shard_map/all_to_all | solution.py:29
  20.7 20.8 %all-to-all-start = ((bf16[128,8,1120]{2,1,0:T(8,128)(2,1)}), bf16[128,8,1120]{2,1,0:T(8,128)(2,1)}, u32[]{:S(2)}, u32[]{:S(2)}) async-start(bf16[128,8,1120]{2,1,0:T(8,128)(2,1)} %all_to_all.18), calls=%async_computation | async-start | bytes 4718592 | tf_op jit(solution)/shard_map/all_to_all | solution.py:29
  46.9 104.3 %all-to-all-done = bf16[128,8,1120]{2,1,0:T(8,128)(2,1)} async-done(((bf16[128,8,1120]{2,1,0:T(8,128)(2,1)}), bf16[128,8,1120]{2,1,0:T(8,128)(2,1)}, u32[]{:S(2)}, u32[]{:S(2)}) %all-to-all-start) | async-done | bytes 2293792 | tf_op jit(solution)/shard_map/all_to_all | solution.py:29
  151.3 4.5 copy.56
  155.8 2.9 slice.111
  158.6 2.2 select_bitcast_fusion.2
  160.8 2.4 collective-permute-start
  163.3 2.3 collective-permute-start.1
  165.6 3.5 collective-permute-start.2
  169.1 3.3 collective-permute-start.3
  174.4 3.9 copy.57
  178.3 5.2 %convolution_convert_fusion = bf16[1024,1024]{1,0:T(8,128)(2,1)} fusion(bf16[1,896,1024]{2,1,0:T(8,128)(2,1)S(1)} %copy-done, bf16[128,8,896]{2,1,0:T(8,128)(2,1)} %copy.57), kind=kOutput, calls=%fused_computation.8 | convolution fusion | flops 1880096768 | bytes 5767168 | tf_op jit(solution)/shard_map/dot_general | solution.py:105
  184.7 4.0 collective-permute-start.5
  194.7 2.6 copy.60
  197.3 3.6 fusion.8
  201.3 49.7 %all_to_all.28 = bf16[4,480,1024]{2,1,0:T(8,128)(2,1)S(1)} all-to-all(bf16[4,480,1024]{2,1,0:T(8,128)(2,1)S(1)} %pad_maximum_fusion), channel_id=1, replica_groups=mesh['expert'=128,'dp'=4] {'dp'}, dimensions={0} | all-to-all | bytes 7864320 | tf_op jit(solution)/shard_map/all_to_all | solution.py:39
  252.9 47.4 %all_to_all.29 = bf16[4,480,1024]{2,1,0:T(8,128)(2,1)S(1)} all-to-all(bf16[4,480,1024]{2,1,0:T(8,128)(2,1)S(1)} %broadcast_in_dim.44), channel_id=1, replica_groups=mesh['expert'=128,'dp'=4] {'dp'}, dimensions={0} | all-to-all | bytes 7864320 | tf_op jit(solution)/shard_map/all_to_all | solution.py:43
  303.7 2.1 fusion.13
  313.7 4.7 collective-permute-start.11
  318.4 3.7 collective-permute-start.6
  322.2 5.2 %collective-permute-start.7 = (bf16[128,896]{0,1:T(8,128)(2,1)}, bf16[128,896]{0,1:T(8,128)(2,1)}, u32[]{:S(2)}, u32[]{:S(2)}) collective-permute-start(bf16[128,896]{0,1:T(8,128)(2,1)} %get-tuple-element.25), channel_id=1, source_target_pairs={{0,384},{4,388},{8,392},{12,396},{16,400},{20,404},{24,408},{28,41... | collective-permute-start | bytes 688136 | tf_op jit(solution)/shard_map/ppermute | solution.py:116
  327.3 2.2 collective-permute-start.8
  331.6 3.6 convert_bitcast_fusion
  335.2 3.1 copy.61
  341.0 4.5 copy.62
  345.5 10.8 %all-to-all-start.3 = ((bf16[128,8,1120]{2,1,0:T(8,128)(2,1)}), bf16[128,8,1120]{2,1,0:T(8,128)(2,1)}, u32[]{:S(2)}, u32[]{:S(2)}) async-start(bf16[128,8,1120]{2,1,0:T(8,128)(2,1)} %copy.62), calls=%async_computation.3 | async-start | bytes 4718592 | tf_op jit(solution)/shard_map/all_to_all | solution.py:29
  358.2 107.9 %all-to-all-done.3 = bf16[128,8,1120]{2,1,0:T(8,128)(2,1)} async-done(((bf16[128,8,1120]{2,1,0:T(8,128)(2,1)}), bf16[128,8,1120]{2,1,0:T(8,128)(2,1)}, u32[]{:S(2)}, u32[]{:S(2)}) %all-to-all-start.3) | async-done | bytes 2293792 | tf_op jit(solution)/shard_map/all_to_all | solution.py:29
  466.1 6.6 %reshape_reshape.7 = bf16[1280,896]{1,0:T(8,128)(2,1)} reshape(bf16[128,8,1120]{2,1,0:T(8,128)(2,1)} %all-to-all-done.3) | data formatting | bytes 4587520 | tf_op jit(solution)/shard_map/reshape;reshape | solution.py:131
  472.7 3.5 convolution_convert_fusion.1
  (80 shorter events, 27.7 us)
Async XLA Ops:
  0.0 178.3 %copy-start = (bf16[1,896,1024]{2,1,0:T(8,128)(2,1)S(1)}, bf16[1,896,1024]{2,1,0:T(8,128)(2,1)}, u32[]{:S(2)}) copy-start(bf16[1,896,1024]{2,1,0:T(8,128)(2,1)} %param.8) | copy-start | bytes 5505028
  0.0 9.6 %copy-start.6 = (bf16[128,896]{1,0:T(8,128)(2,1)S(1)}, bf16[128,896]{1,0:T(8,128)(2,1)}, u32[]{:S(2)}) copy-start(bf16[128,896]{1,0:T(8,128)(2,1)} %param.5) | copy-start | bytes 688132
  20.7 130.6 %all-to-all-start = ((bf16[128,8,1120]{2,1,0:T(8,128)(2,1)}), bf16[128,8,1120]{2,1,0:T(8,128)(2,1)}, u32[]{:S(2)}, u32[]{:S(2)}) async-start(bf16[128,8,1120]{2,1,0:T(8,128)(2,1)} %all_to_all.18), calls=%async_computation | async-start | bytes 4718592 | tf_op jit(solution)/shard_map/all_to_all | solution.py:29
  160.8 23.8 %collective-permute-start = (bf16[128,896]{0,1:T(8,128)(2,1)}, bf16[128,896]{0,1:T(8,128)(2,1)}, u32[]{:S(2)}, u32[]{:S(2)}) collective-permute-start(bf16[128,896]{0,1:T(8,128)(2,1)} %get-tuple-element.20), channel_id=1, source_target_pairs={{4,0},{0,4},{12,8},{8,12},{20,16},{16,20},{28,24},{24,28},{36,32},... | collective-permute-start | bytes 688136 | tf_op jit(solution)/shard_map/ppermute | solution.py:101
  163.3 26.4 %collective-permute-start.1 = (bf16[128,896]{0,1:T(8,128)(2,1)}, bf16[128,896]{0,1:T(8,128)(2,1)}, u32[]{:S(2)}, u32[]{:S(2)}) collective-permute-start(bf16[128,896]{0,1:T(8,128)(2,1)} %get-tuple-element.16), channel_id=1, source_target_pairs={{8,0},{12,4},{16,8},{20,12},{24,16},{28,20},{32,24},{36,28},{40,32... | collective-permute-start | bytes 688136 | tf_op jit(solution)/shard_map/ppermute | solution.py:101
  165.6 25.1 %collective-permute-start.2 = (bf16[128,896]{0,1:T(8,128)(2,1)}, bf16[128,896]{0,1:T(8,128)(2,1)}, u32[]{:S(2)}, u32[]{:S(2)}) collective-permute-start(bf16[128,896]{0,1:T(8,128)(2,1)} %get-tuple-element.17), channel_id=1, source_target_pairs={{120,0},{124,4},{0,8},{4,12},{8,16},{12,20},{16,24},{20,28},{24,32... | collective-permute-start | bytes 688136 | tf_op jit(solution)/shard_map/ppermute | solution.py:101
  169.1 22.5 %collective-permute-start.3 = (bf16[128,896]{0,1:T(8,128)(2,1)}, bf16[128,896]{0,1:T(8,128)(2,1)}, u32[]{:S(2)}, u32[]{:S(2)}) collective-permute-start(bf16[128,896]{0,1:T(8,128)(2,1)} %get-tuple-element.18), channel_id=1, source_target_pairs={{128,0},{132,4},{136,8},{140,12},{144,16},{148,20},{152,24},{156,2... | collective-permute-start | bytes 688136 | tf_op jit(solution)/shard_map/ppermute | solution.py:101
  172.4 20.2 %collective-permute-start.4 = (bf16[128,896]{0,1:T(8,128)(2,1)}, bf16[128,896]{0,1:T(8,128)(2,1)}, u32[]{:S(2)}, u32[]{:S(2)}) collective-permute-start(bf16[128,896]{0,1:T(8,128)(2,1)} %get-tuple-element.19), channel_id=1, source_target_pairs={{384,0},{388,4},{392,8},{396,12},{400,16},{404,20},{408,24},{412,2... | collective-permute-start | bytes 688136 | tf_op jit(solution)/shard_map/ppermute | solution.py:101
  178.3 6.3 %copy-start.7 = (bf16[128,896]{0,1:T(8,128)(2,1)S(1)}, bf16[128,896]{0,1:T(8,128)(2,1)}, u32[]{:S(2)}) copy-start(bf16[128,896]{0,1:T(8,128)(2,1)} %get-tuple-element.15) | copy-start | bytes 688132
  184.7 10.0 %collective-permute-start.5 = (bf16[128,896]{0,1:T(8,128)(2,1)S(1)}, bf16[128,896]{0,1:T(8,128)(2,1)S(1)}, u32[]{:S(2)}, u32[]{:S(2)}) collective-permute-start(bf16[128,896]{0,1:T(8,128)(2,1)S(1)} %copy-done.7), channel_id=1, source_target_pairs={{12,0},{8,4},{20,8},{16,12},{28,16},{24,20},{36,24},{32,28},{44,32... | collective-permute-start | bytes 688136 | tf_op jit(solution)/shard_map/ppermute | solution.py:101
  197.3 3.6 copy-start.3
  300.3 1.9 copy-start.2
  302.2 1.5 copy-start.9
  307.0 22.6 %collective-permute-start.10 = (bf16[128,896]{0,1:T(8,128)(2,1)S(1)}, bf16[128,896]{0,1:T(8,128)(2,1)S(1)}, u32[]{:S(2)}, u32[]{:S(2)}) collective-permute-start(bf16[128,896]{0,1:T(8,128)(2,1)S(1)} %get-tuple-element.22), channel_id=1, source_target_pairs={{0,8},{4,12},{8,16},{12,20},{16,24},{20,28},{24,32},{28,36},{32,40... | collective-permute-start | bytes 688136 | tf_op jit(solution)/shard_map/ppermute | solution.py:116
  313.7 24.6 %collective-permute-start.11 = (bf16[128,896]{0,1:T(8,128)(2,1)}, bf16[128,896]{0,1:T(8,128)(2,1)}, u32[]{:S(2)}, u32[]{:S(2)}) collective-permute-start(bf16[128,896]{0,1:T(8,128)(2,1)} %get-tuple-element.21), channel_id=1, source_target_pairs={{0,4},{4,0},{8,12},{12,8},{16,20},{20,16},{24,28},{28,24},{32,36},... | collective-permute-start | bytes 688136 | tf_op jit(solution)/shard_map/ppermute | solution.py:116
  318.4 19.9 %collective-permute-start.6 = (bf16[128,896]{0,1:T(8,128)(2,1)}, bf16[128,896]{0,1:T(8,128)(2,1)}, u32[]{:S(2)}, u32[]{:S(2)}) collective-permute-start(bf16[128,896]{0,1:T(8,128)(2,1)} %get-tuple-element.26), channel_id=1, source_target_pairs={{0,12},{4,8},{8,20},{12,16},{16,28},{20,24},{24,36},{28,32},{32,44... | collective-permute-start | bytes 688136 | tf_op jit(solution)/shard_map/ppermute | solution.py:116
  322.2 16.2 %collective-permute-start.7 = (bf16[128,896]{0,1:T(8,128)(2,1)}, bf16[128,896]{0,1:T(8,128)(2,1)}, u32[]{:S(2)}, u32[]{:S(2)}) collective-permute-start(bf16[128,896]{0,1:T(8,128)(2,1)} %get-tuple-element.25), channel_id=1, source_target_pairs={{0,384},{4,388},{8,392},{12,396},{16,400},{20,404},{24,408},{28,41... | collective-permute-start | bytes 688136 | tf_op jit(solution)/shard_map/ppermute | solution.py:116
  327.3 4.2 slice-start
  327.3 4.2 copy-start.10
  327.3 11.0 %collective-permute-start.8 = (bf16[128,896]{0,1:T(8,128)(2,1)}, bf16[128,896]{0,1:T(8,128)(2,1)}, u32[]{:S(2)}, u32[]{:S(2)}) collective-permute-start(bf16[128,896]{0,1:T(8,128)(2,1)} %get-tuple-element.24), channel_id=1, source_target_pairs={{0,128},{4,132},{8,136},{12,140},{16,144},{20,148},{24,152},{28,15... | collective-permute-start | bytes 688136 | tf_op jit(solution)/shard_map/ppermute | solution.py:116
  329.5 2.0 copy-start.4
  329.6 8.9 %collective-permute-start.9 = (bf16[128,896]{0,1:T(8,128)(2,1)}, bf16[128,896]{0,1:T(8,128)(2,1)}, u32[]{:S(2)}, u32[]{:S(2)}) collective-permute-start(bf16[128,896]{0,1:T(8,128)(2,1)} %get-tuple-element.23), channel_id=1, source_target_pairs={{0,120},{4,124},{8,0},{12,4},{16,8},{20,12},{24,16},{28,20},{32,24... | collective-permute-start | bytes 688136 | tf_op jit(solution)/shard_map/ppermute | solution.py:116
  338.3 0.9 copy-start.5
  345.5 10.9 %copy-start.8 = (f32[128,8]{0,1:T(8,128)S(1)}, f32[128,8]{0,1:T(8,128)}, u32[]{:S(2)}) copy-start(f32[128,8]{0,1:T(8,128)} %param.7) | copy-start | bytes 12292
  345.5 120.6 %all-to-all-start.3 = ((bf16[128,8,1120]{2,1,0:T(8,128)(2,1)}), bf16[128,8,1120]{2,1,0:T(8,128)(2,1)}, u32[]{:S(2)}, u32[]{:S(2)}) async-start(bf16[128,8,1120]{2,1,0:T(8,128)(2,1)} %copy.62), calls=%async_computation.3 | async-start | bytes 4718592 | tf_op jit(solution)/shard_map/all_to_all | solution.py:29
  466.1 10.2 %copy-start.1 = (bf16[1,896,1024]{2,1,0:T(8,128)(2,1)S(1)}, bf16[1,896,1024]{2,1,0:T(8,128)(2,1)}, u32[]{:S(2)}) copy-start(bf16[1,896,1024]{2,1,0:T(8,128)(2,1)} %param.8) | copy-start | bytes 5505028

commit v7 on v6

--- a/solution.py
+++ b/solution.py
@@ -88,7 +88,9 @@
     mix_weights = gate_scores * (ROUTE_SCALE / jnp.sum(gate_scores, axis=1, keepdims=True))
     send_table = jnp.full((experts * slots,), row_total, jnp.int32)
     send_table = send_table.at[position].set(jnp.arange(row_total, dtype=jnp.int32), mode="drop")
-    sending = padded[send_table // chosen_count]
+    token_range = jnp.arange(token_count, dtype=jnp.int32)
+    picks = ((send_table // chosen_count)[:, None] == token_range[None, :]).astype(tokens.dtype)
+    sending = jnp.dot(picks, tokens, preferred_element_type=jnp.float32).astype(tokens.dtype)
     arrived = exchange(sending, experts).reshape(experts, slots, features)
 
     mine = jnp.where(me == hot_ids[0], 0, 1)

time: 478 us -> 475 us (level)
  local copies, waits for them, and re-layouts: 56.2 us -> 51.3 us
    gather x1 -> x0, local copies, waits for them, and re-layouts: 4.97 us -> none  [local(): sending = padded[send_table // chosen_count]]
where the time goes in v7:
time: 475 us; the launch traced here: 474 us
  waiting for transfers between devices  213 us (45%)
  blocking collectives  97.1 us (20%)
  starting transfers between devices  69 us (15%)
  local copies, waits for them, and re-layouts  51.3 us (11%)
  matrix products  20.3 us (4%)
  other arithmetic  12.5 us (3%)
  between operations  10.1 us (2%)
    all_to_all x2, waiting for transfers between devices, exchange(): lax.all_to_all(packed, 'expert', split_axis=0, concat_axis=0, tiled=True)  212 us
    all_to_all x1, blocking collectives, silu_hidden(): parts = lax.all_to_all(blocks, 'dp', 0, 0, tiled=True)  49.7 us
    all_to_all x1, blocking collectives, silu_hidden(): gathered = lax.all_to_all(spread, 'dp', 0, 0, tiled=True)  47.4 us
    all_to_all x2, starting transfers between devices, exchange(): lax.all_to_all(packed, 'expert', split_axis=0, concat_axis=0, tiled=True)  31.8 us
    ppermute x6, starting transfers between devices, local(): back.append(lax.ppermute(hot_out[i], 'expert', pairs))  19.7 us
    ppermute x6, starting transfers between devices, local(): hot_rows.append(lax.ppermute(outgoing, 'expert', pairs))  17.5 us
    all_to_all x3, local copies, waits for them, and re-layouts, exchange(): lax.all_to_all(packed, 'expert', split_axis=0, concat_axis=0, tiled=True)  15 us
    unnamed x28, local copies, waits for them, and re-layouts  9.77 us
  transfers between devices with their start and end apart: 14, of which 4 were waited for; matrix products, arithmetic and copies ran while one was open for 5% of the time, Pallas kernels for 0%

profile of v7, /device:TPU:1, one launch (start us, length us, event | category | flops | bytes accessed | tf_op | source)
XLA Modules:
  0.0 473.6 jit_solution(10178942556367042771)
XLA Ops:
  2.0 2.5 top_k.11
  5.3 4.3 scatter_custom_fusion
  9.6 2.2 convolution_convert_fusion
  11.8 6.0 %all_to_all.18 = bf16[128,8,1120]{2,1,0:T(8,128)(2,1)} reshape(bf16[1280,896]{1,0:T(8,128)(2,1)} %convolution_convert_fusion) | data formatting | bytes 4587520 | tf_op jit(solution)/shard_map/all_to_all | solution.py:29
  17.8 20.8 %all-to-all-start = ((bf16[128,8,1120]{2,1,0:T(8,128)(2,1)}), bf16[128,8,1120]{2,1,0:T(8,128)(2,1)}, u32[]{:S(2)}, u32[]{:S(2)}) async-start(bf16[128,8,1120]{2,1,0:T(8,128)(2,1)} %all_to_all.18), calls=%async_computation | async-start | bytes 4718592 | tf_op jit(solution)/shard_map/all_to_all | solution.py:29
  44.1 104.3 %all-to-all-done = bf16[128,8,1120]{2,1,0:T(8,128)(2,1)} async-done(((bf16[128,8,1120]{2,1,0:T(8,128)(2,1)}), bf16[128,8,1120]{2,1,0:T(8,128)(2,1)}, u32[]{:S(2)}, u32[]{:S(2)}) %all-to-all-start) | async-done | bytes 2293792 | tf_op jit(solution)/shard_map/all_to_all | solution.py:29
  148.4 4.5 copy.56
  152.9 2.9 slice.109
  155.8 2.2 select_bitcast_fusion.2
  158.0 2.4 collective-permute-start
  160.5 2.3 collective-permute-start.1
  162.7 3.5 collective-permute-start.2
  166.3 3.3 collective-permute-start.3
  171.6 3.9 copy.57
  175.5 5.2 %convolution_convert_fusion.1 = bf16[1024,1024]{1,0:T(8,128)(2,1)} fusion(bf16[1,896,1024]{2,1,0:T(8,128)(2,1)S(1)} %copy-done, bf16[128,8,896]{2,1,0:T(8,128)(2,1)} %copy.57), kind=kOutput, calls=%fused_computation.8 | convolution fusion | flops 1880096768 | bytes 5767168 | tf_op jit(solution)/shard_map/dot_general | solution.py:107
  181.9 4.0 collective-permute-start.5
  191.9 2.6 copy.60
  194.4 3.6 fusion.8
  198.5 49.7 %all_to_all.28 = bf16[4,480,1024]{2,1,0:T(8,128)(2,1)S(1)} all-to-all(bf16[4,480,1024]{2,1,0:T(8,128)(2,1)S(1)} %pad_maximum_fusion), channel_id=1, replica_groups=mesh['expert'=128,'dp'=4] {'dp'}, dimensions={0} | all-to-all | bytes 7864320 | tf_op jit(solution)/shard_map/all_to_all | solution.py:39
  250.1 47.4 %all_to_all.29 = bf16[4,480,1024]{2,1,0:T(8,128)(2,1)S(1)} all-to-all(bf16[4,480,1024]{2,1,0:T(8,128)(2,1)S(1)} %broadcast_in_dim.41), channel_id=1, replica_groups=mesh['expert'=128,'dp'=4] {'dp'}, dimensions={0} | all-to-all | bytes 7864320 | tf_op jit(solution)/shard_map/all_to_all | solution.py:43
  300.9 2.1 fusion.13
  310.9 4.7 collective-permute-start.11
  315.6 3.7 collective-permute-start.6
  319.3 5.1 %collective-permute-start.7 = (bf16[128,896]{0,1:T(8,128)(2,1)}, bf16[128,896]{0,1:T(8,128)(2,1)}, u32[]{:S(2)}, u32[]{:S(2)}) collective-permute-start(bf16[128,896]{0,1:T(8,128)(2,1)} %get-tuple-element.25), channel_id=1, source_target_pairs={{0,384},{4,388},{8,392},{12,396},{16,400},{20,404},{24,408},{28,41... | collective-permute-start | bytes 688136 | tf_op jit(solution)/shard_map/ppermute | solution.py:118
  324.5 2.2 collective-permute-start.8
  328.8 3.6 convert_bitcast_fusion
  332.3 3.1 copy.61
  338.2 4.5 copy.62
  342.6 11.0 %all-to-all-start.3 = ((bf16[128,8,1120]{2,1,0:T(8,128)(2,1)}), bf16[128,8,1120]{2,1,0:T(8,128)(2,1)}, u32[]{:S(2)}, u32[]{:S(2)}) async-start(bf16[128,8,1120]{2,1,0:T(8,128)(2,1)} %copy.62), calls=%async_computation.3 | async-start | bytes 4718592 | tf_op jit(solution)/shard_map/all_to_all | solution.py:29
  355.6 107.9 %all-to-all-done.3 = bf16[128,8,1120]{2,1,0:T(8,128)(2,1)} async-done(((bf16[128,8,1120]{2,1,0:T(8,128)(2,1)}), bf16[128,8,1120]{2,1,0:T(8,128)(2,1)}, u32[]{:S(2)}, u32[]{:S(2)}) %all-to-all-start.3) | async-done | bytes 2293792 | tf_op jit(solution)/shard_map/all_to_all | solution.py:29
  463.5 6.6 %reshape_reshape.7 = bf16[1280,896]{1,0:T(8,128)(2,1)} reshape(bf16[128,8,1120]{2,1,0:T(8,128)(2,1)} %all-to-all-done.3) | data formatting | bytes 4587520 | tf_op jit(solution)/shard_map/reshape;reshape | solution.py:133
  470.1 3.5 convolution_convert_fusion.2
  (78 shorter events, 27.6 us)
Async XLA Ops:
  0.0 175.5 %copy-start = (bf16[1,896,1024]{2,1,0:T(8,128)(2,1)S(1)}, bf16[1,896,1024]{2,1,0:T(8,128)(2,1)}, u32[]{:S(2)}) copy-start(bf16[1,896,1024]{2,1,0:T(8,128)(2,1)} %param.8) | copy-start | bytes 5505028
  0.0 9.6 %copy-start.6 = (bf16[128,896]{1,0:T(8,128)(2,1)S(1)}, bf16[128,896]{1,0:T(8,128)(2,1)}, u32[]{:S(2)}) copy-start(bf16[128,896]{1,0:T(8,128)(2,1)} %param.5) | copy-start | bytes 688132
  17.8 130.6 %all-to-all-start = ((bf16[128,8,1120]{2,1,0:T(8,128)(2,1)}), bf16[128,8,1120]{2,1,0:T(8,128)(2,1)}, u32[]{:S(2)}, u32[]{:S(2)}) async-start(bf16[128,8,1120]{2,1,0:T(8,128)(2,1)} %all_to_all.18), calls=%async_computation | async-start | bytes 4718592 | tf_op jit(solution)/shard_map/all_to_all | solution.py:29
  158.0 23.8 %collective-permute-start = (bf16[128,896]{0,1:T(8,128)(2,1)}, bf16[128,896]{0,1:T(8,128)(2,1)}, u32[]{:S(2)}, u32[]{:S(2)}) collective-permute-start(bf16[128,896]{0,1:T(8,128)(2,1)} %get-tuple-element.20), channel_id=1, source_target_pairs={{4,0},{0,4},{12,8},{8,12},{20,16},{16,20},{28,24},{24,28},{36,32},... | collective-permute-start | bytes 688136 | tf_op jit(solution)/shard_map/ppermute | solution.py:103
  160.5 26.4 %collective-permute-start.1 = (bf16[128,896]{0,1:T(8,128)(2,1)}, bf16[128,896]{0,1:T(8,128)(2,1)}, u32[]{:S(2)}, u32[]{:S(2)}) collective-permute-start(bf16[128,896]{0,1:T(8,128)(2,1)} %get-tuple-element.16), channel_id=1, source_target_pairs={{8,0},{12,4},{16,8},{20,12},{24,16},{28,20},{32,24},{36,28},{40,32... | collective-permute-start | bytes 688136 | tf_op jit(solution)/shard_map/ppermute | solution.py:103
  162.7 25.1 %collective-permute-start.2 = (bf16[128,896]{0,1:T(8,128)(2,1)}, bf16[128,896]{0,1:T(8,128)(2,1)}, u32[]{:S(2)}, u32[]{:S(2)}) collective-permute-start(bf16[128,896]{0,1:T(8,128)(2,1)} %get-tuple-element.17), channel_id=1, source_target_pairs={{120,0},{124,4},{0,8},{4,12},{8,16},{12,20},{16,24},{20,28},{24,32... | collective-permute-start | bytes 688136 | tf_op jit(solution)/shard_map/ppermute | solution.py:103
  166.3 22.5 %collective-permute-start.3 = (bf16[128,896]{0,1:T(8,128)(2,1)}, bf16[128,896]{0,1:T(8,128)(2,1)}, u32[]{:S(2)}, u32[]{:S(2)}) collective-permute-start(bf16[128,896]{0,1:T(8,128)(2,1)} %get-tuple-element.18), channel_id=1, source_target_pairs={{128,0},{132,4},{136,8},{140,12},{144,16},{148,20},{152,24},{156,2... | collective-permute-start | bytes 688136 | tf_op jit(solution)/shard_map/ppermute | solution.py:103
  169.5 20.2 %collective-permute-start.4 = (bf16[128,896]{0,1:T(8,128)(2,1)}, bf16[128,896]{0,1:T(8,128)(2,1)}, u32[]{:S(2)}, u32[]{:S(2)}) collective-permute-start(bf16[128,896]{0,1:T(8,128)(2,1)} %get-tuple-element.19), channel_id=1, source_target_pairs={{384,0},{388,4},{392,8},{396,12},{400,16},{404,20},{408,24},{412,2... | collective-permute-start | bytes 688136 | tf_op jit(solution)/shard_map/ppermute | solution.py:103
  175.5 6.3 %copy-start.7 = (bf16[128,896]{0,1:T(8,128)(2,1)S(1)}, bf16[128,896]{0,1:T(8,128)(2,1)}, u32[]{:S(2)}) copy-start(bf16[128,896]{0,1:T(8,128)(2,1)} %get-tuple-element.15) | copy-start | bytes 688132
  181.9 10.0 %collective-permute-start.5 = (bf16[128,896]{0,1:T(8,128)(2,1)S(1)}, bf16[128,896]{0,1:T(8,128)(2,1)S(1)}, u32[]{:S(2)}, u32[]{:S(2)}) collective-permute-start(bf16[128,896]{0,1:T(8,128)(2,1)S(1)} %copy-done.7), channel_id=1, source_target_pairs={{12,0},{8,4},{20,8},{16,12},{28,16},{24,20},{36,24},{32,28},{44,32... | collective-permute-start | bytes 688136 | tf_op jit(solution)/shard_map/ppermute | solution.py:103
  194.4 3.6 copy-start.3
  297.5 1.9 copy-start.2
  299.4 1.5 copy-start.9
  304.1 22.6 %collective-permute-start.10 = (bf16[128,896]{0,1:T(8,128)(2,1)S(1)}, bf16[128,896]{0,1:T(8,128)(2,1)S(1)}, u32[]{:S(2)}, u32[]{:S(2)}) collective-permute-start(bf16[128,896]{0,1:T(8,128)(2,1)S(1)} %get-tuple-element.22), channel_id=1, source_target_pairs={{0,8},{4,12},{8,16},{12,20},{16,24},{20,28},{24,32},{28,36},{32,40... | collective-permute-start | bytes 688136 | tf_op jit(solution)/shard_map/ppermute | solution.py:118
  310.9 24.6 %collective-permute-start.11 = (bf16[128,896]{0,1:T(8,128)(2,1)}, bf16[128,896]{0,1:T(8,128)(2,1)}, u32[]{:S(2)}, u32[]{:S(2)}) collective-permute-start(bf16[128,896]{0,1:T(8,128)(2,1)} %get-tuple-element.21), channel_id=1, source_target_pairs={{0,4},{4,0},{8,12},{12,8},{16,20},{20,16},{24,28},{28,24},{32,36},... | collective-permute-start | bytes 688136 | tf_op jit(solution)/shard_map/ppermute | solution.py:118
  315.6 19.9 %collective-permute-start.6 = (bf16[128,896]{0,1:T(8,128)(2,1)}, bf16[128,896]{0,1:T(8,128)(2,1)}, u32[]{:S(2)}, u32[]{:S(2)}) collective-permute-start(bf16[128,896]{0,1:T(8,128)(2,1)} %get-tuple-element.26), channel_id=1, source_target_pairs={{0,12},{4,8},{8,20},{12,16},{16,28},{20,24},{24,36},{28,32},{32,44... | collective-permute-start | bytes 688136 | tf_op jit(solution)/shard_map/ppermute | solution.py:118
  319.3 16.2 %collective-permute-start.7 = (bf16[128,896]{0,1:T(8,128)(2,1)}, bf16[128,896]{0,1:T(8,128)(2,1)}, u32[]{:S(2)}, u32[]{:S(2)}) collective-permute-start(bf16[128,896]{0,1:T(8,128)(2,1)} %get-tuple-element.25), channel_id=1, source_target_pairs={{0,384},{4,388},{8,392},{12,396},{16,400},{20,404},{24,408},{28,41... | collective-permute-start | bytes 688136 | tf_op jit(solution)/shard_map/ppermute | solution.py:118
  324.5 4.2 slice-start
  324.5 4.2 copy-start.10
  324.5 11.0 %collective-permute-start.8 = (bf16[128,896]{0,1:T(8,128)(2,1)}, bf16[128,896]{0,1:T(8,128)(2,1)}, u32[]{:S(2)}, u32[]{:S(2)}) collective-permute-start(bf16[128,896]{0,1:T(8,128)(2,1)} %get-tuple-element.24), channel_id=1, source_target_pairs={{0,128},{4,132},{8,136},{12,140},{16,144},{20,148},{24,152},{28,15... | collective-permute-start | bytes 688136 | tf_op jit(solution)/shard_map/ppermute | solution.py:118
  326.7 2.0 copy-start.4
  326.7 8.9 %collective-permute-start.9 = (bf16[128,896]{0,1:T(8,128)(2,1)}, bf16[128,896]{0,1:T(8,128)(2,1)}, u32[]{:S(2)}, u32[]{:S(2)}) collective-permute-start(bf16[128,896]{0,1:T(8,128)(2,1)} %get-tuple-element.23), channel_id=1, source_target_pairs={{0,120},{4,124},{8,0},{12,4},{16,8},{20,12},{24,16},{28,20},{32,24... | collective-permute-start | bytes 688136 | tf_op jit(solution)/shard_map/ppermute | solution.py:118
  335.5 0.9 copy-start.5
  342.6 11.1 %copy-start.8 = (f32[128,8]{0,1:T(8,128)S(1)}, f32[128,8]{0,1:T(8,128)}, u32[]{:S(2)}) copy-start(f32[128,8]{0,1:T(8,128)} %param.7) | copy-start | bytes 12292
  342.6 120.8 %all-to-all-start.3 = ((bf16[128,8,1120]{2,1,0:T(8,128)(2,1)}), bf16[128,8,1120]{2,1,0:T(8,128)(2,1)}, u32[]{:S(2)}, u32[]{:S(2)}) async-start(bf16[128,8,1120]{2,1,0:T(8,128)(2,1)} %copy.62), calls=%async_computation.3 | async-start | bytes 4718592 | tf_op jit(solution)/shard_map/all_to_all | solution.py:29
  463.5 10.2 %copy-start.1 = (bf16[1,896,1024]{2,1,0:T(8,128)(2,1)S(1)}, bf16[1,896,1024]{2,1,0:T(8,128)(2,1)}, u32[]{:S(2)}) copy-start(bf16[1,896,1024]{2,1,0:T(8,128)(2,1)} %param.8) | copy-start | bytes 5505028

commit v8 on v7

--- a/solution.py
+++ b/solution.py
@@ -94,7 +94,7 @@
     arrived = exchange(sending, experts).reshape(experts, slots, features)
 
     mine = jnp.where(me == hot_ids[0], 0, 1)
-    own_extra = jnp.where(mine == 0, arrived[:, cold_most], arrived[:, cold_most + 1])
+    own_extra = lax.dynamic_index_in_dim(arrived, cold_most + mine, axis=1, keepdims=False)
     hot_rows = [own_extra]
     for i in range(1, extra):
         owner = moved(me, relays[i], experts, -1)

time: 475 us -> 475 us (level)
    unnamed x28 -> x29, local copies, waits for them, and re-layouts: 9.77 us -> 10.7 us
where the time goes in v8:
time: 475 us; the launch traced here: 473 us
  waiting for transfers between devices  213 us (45%)
  blocking collectives  97.1 us (20%)
  starting transfers between devices  68.8 us (14%)
  local copies, waits for them, and re-layouts  52.2 us (11%)
  matrix products  20.3 us (4%)
  other arithmetic  11.4 us (2%)
  between operations  10.1 us (2%)
    all_to_all x2, waiting for transfers between devices, exchange(): lax.all_to_all(packed, 'expert', split_axis=0, concat_axis=0, tiled=True)  212 us
    all_to_all x1, blocking collectives, silu_hidden(): parts = lax.all_to_all(blocks, 'dp', 0, 0, tiled=True)  49.7 us
    all_to_all x1, blocking collectives, silu_hidden(): gathered = lax.all_to_all(spread, 'dp', 0, 0, tiled=True)  47.4 us
    all_to_all x2, starting transfers between devices, exchange(): lax.all_to_all(packed, 'expert', split_axis=0, concat_axis=0, tiled=True)  31.6 us
    ppermute x6, starting transfers between devices, local(): back.append(lax.ppermute(hot_out[i], 'expert', pairs))  19.7 us
    ppermute x6, starting transfers between devices, local(): hot_rows.append(lax.ppermute(outgoing, 'expert', pairs))  17.5 us
    all_to_all x3, local copies, waits for them, and re-layouts, exchange(): lax.all_to_all(packed, 'expert', split_axis=0, concat_axis=0, tiled=True)  15 us
    unnamed x29, local copies, waits for them, and re-layouts  10.7 us
  transfers between devices with their start and end apart: 14, of which 4 were waited for; matrix products, arithmetic and copies ran while one was open for 5% of the time, Pallas kernels for 0%

profile of v8, /device:TPU:1, one launch (start us, length us, event | category | flops | bytes accessed | tf_op | source)
XLA Modules:
  0.0 473.3 jit_solution(3638226720853916901)
XLA Ops:
  2.0 2.5 top_k.11
  5.3 4.3 scatter_custom_fusion
  9.6 2.2 convolution_convert_fusion
  11.8 6.0 %all_to_all.18 = bf16[128,8,1120]{2,1,0:T(8,128)(2,1)} reshape(bf16[1280,896]{1,0:T(8,128)(2,1)} %convolution_convert_fusion) | data formatting | bytes 4587520 | tf_op jit(solution)/shard_map/all_to_all | solution.py:29
  17.8 20.8 %all-to-all-start = ((bf16[128,8,1120]{2,1,0:T(8,128)(2,1)}), bf16[128,8,1120]{2,1,0:T(8,128)(2,1)}, u32[]{:S(2)}, u32[]{:S(2)}) async-start(bf16[128,8,1120]{2,1,0:T(8,128)(2,1)} %all_to_all.18), calls=%async_computation | async-start | bytes 4718592 | tf_op jit(solution)/shard_map/all_to_all | solution.py:29
  44.1 104.3 %all-to-all-done = bf16[128,8,1120]{2,1,0:T(8,128)(2,1)} async-done(((bf16[128,8,1120]{2,1,0:T(8,128)(2,1)}), bf16[128,8,1120]{2,1,0:T(8,128)(2,1)}, u32[]{:S(2)}, u32[]{:S(2)}) %all-to-all-start) | async-done | bytes 2293792 | tf_op jit(solution)/shard_map/all_to_all | solution.py:29
  148.4 4.5 copy.61
  152.9 2.9 slice.107
  155.8 2.2 select_bitcast_fusion.2
  158.0 2.4 collective-permute-start
  160.5 2.3 collective-permute-start.1
  162.8 3.5 collective-permute-start.2
  166.3 3.3 collective-permute-start.3
  171.6 3.9 copy.62
  175.5 5.2 %convolution_convert_fusion.1 = bf16[1024,1024]{1,0:T(8,128)(2,1)} fusion(bf16[1,896,1024]{2,1,0:T(8,128)(2,1)S(1)} %copy-done, bf16[128,8,896]{2,1,0:T(8,128)(2,1)} %copy.62), kind=kOutput, calls=%fused_computation.8 | convolution fusion | flops 1880096768 | bytes 5767168 | tf_op jit(solution)/shard_map/dot_general | solution.py:107
  181.7 4.0 collective-permute-start.5
  191.7 2.6 copy.67
  194.3 3.6 fusion.8
  198.4 49.7 %all_to_all.28 = bf16[4,480,1024]{2,1,0:T(8,128)(2,1)S(1)} all-to-all(bf16[4,480,1024]{2,1,0:T(8,128)(2,1)S(1)} %pad_maximum_fusion), channel_id=1, replica_groups=mesh['expert'=128,'dp'=4] {'dp'}, dimensions={0} | all-to-all | bytes 7864320 | tf_op jit(solution)/shard_map/all_to_all | solution.py:39
  249.9 47.4 %all_to_all.29 = bf16[4,480,1024]{2,1,0:T(8,128)(2,1)S(1)} all-to-all(bf16[4,480,1024]{2,1,0:T(8,128)(2,1)S(1)} %broadcast_in_dim.41), channel_id=1, replica_groups=mesh['expert'=128,'dp'=4] {'dp'}, dimensions={0} | all-to-all | bytes 7864320 | tf_op jit(solution)/shard_map/all_to_all | solution.py:43
  300.8 2.1 fusion.13
  310.7 4.7 collective-permute-start.11
  315.5 3.7 collective-permute-start.6
  319.2 5.1 %collective-permute-start.7 = (bf16[128,896]{0,1:T(8,128)(2,1)}, bf16[128,896]{0,1:T(8,128)(2,1)}, u32[]{:S(2)}, u32[]{:S(2)}) collective-permute-start(bf16[128,896]{0,1:T(8,128)(2,1)} %get-tuple-element.25), channel_id=1, source_target_pairs={{0,384},{4,388},{8,392},{12,396},{16,400},{20,404},{24,408},{28,41... | collective-permute-start | bytes 688136 | tf_op jit(solution)/shard_map/ppermute | solution.py:118
  324.4 2.2 collective-permute-start.8
  328.6 3.6 convert_bitcast_fusion
  332.2 3.1 copy.68
  338.0 4.5 copy.69
  342.5 10.8 %all-to-all-start.3 = ((bf16[128,8,1120]{2,1,0:T(8,128)(2,1)}), bf16[128,8,1120]{2,1,0:T(8,128)(2,1)}, u32[]{:S(2)}, u32[]{:S(2)}) async-start(bf16[128,8,1120]{2,1,0:T(8,128)(2,1)} %copy.69), calls=%async_computation.3 | async-start | bytes 4718592 | tf_op jit(solution)/shard_map/all_to_all | solution.py:29
  355.2 107.9 %all-to-all-done.3 = bf16[128,8,1120]{2,1,0:T(8,128)(2,1)} async-done(((bf16[128,8,1120]{2,1,0:T(8,128)(2,1)}), bf16[128,8,1120]{2,1,0:T(8,128)(2,1)}, u32[]{:S(2)}, u32[]{:S(2)}) %all-to-all-start.3) | async-done | bytes 2293792 | tf_op jit(solution)/shard_map/all_to_all | solution.py:29
  463.1 6.6 %reshape_reshape.7 = bf16[1280,896]{1,0:T(8,128)(2,1)} reshape(bf16[128,8,1120]{2,1,0:T(8,128)(2,1)} %all-to-all-done.3) | data formatting | bytes 4587520 | tf_op jit(solution)/shard_map/reshape;reshape | solution.py:133
  469.8 3.5 convolution_convert_fusion.2
  (78 shorter events, 27.5 us)
Async XLA Ops:
  0.0 175.5 %copy-start = (bf16[1,896,1024]{2,1,0:T(8,128)(2,1)S(1)}, bf16[1,896,1024]{2,1,0:T(8,128)(2,1)}, u32[]{:S(2)}) copy-start(bf16[1,896,1024]{2,1,0:T(8,128)(2,1)} %param.8) | copy-start | bytes 5505028
  0.0 9.6 %copy-start.6 = (bf16[128,896]{1,0:T(8,128)(2,1)S(1)}, bf16[128,896]{1,0:T(8,128)(2,1)}, u32[]{:S(2)}) copy-start(bf16[128,896]{1,0:T(8,128)(2,1)} %param.5) | copy-start | bytes 688132
  17.8 130.6 %all-to-all-start = ((bf16[128,8,1120]{2,1,0:T(8,128)(2,1)}), bf16[128,8,1120]{2,1,0:T(8,128)(2,1)}, u32[]{:S(2)}, u32[]{:S(2)}) async-start(bf16[128,8,1120]{2,1,0:T(8,128)(2,1)} %all_to_all.18), calls=%async_computation | async-start | bytes 4718592 | tf_op jit(solution)/shard_map/all_to_all | solution.py:29
  158.0 23.7 %collective-permute-start = (bf16[128,896]{0,1:T(8,128)(2,1)}, bf16[128,896]{0,1:T(8,128)(2,1)}, u32[]{:S(2)}, u32[]{:S(2)}) collective-permute-start(bf16[128,896]{0,1:T(8,128)(2,1)} %get-tuple-element.19), channel_id=1, source_target_pairs={{4,0},{0,4},{12,8},{8,12},{20,16},{16,20},{28,24},{24,28},{36,32},... | collective-permute-start | bytes 688136 | tf_op jit(solution)/shard_map/ppermute | solution.py:103
  160.5 26.2 %collective-permute-start.1 = (bf16[128,896]{0,1:T(8,128)(2,1)}, bf16[128,896]{0,1:T(8,128)(2,1)}, u32[]{:S(2)}, u32[]{:S(2)}) collective-permute-start(bf16[128,896]{0,1:T(8,128)(2,1)} %get-tuple-element.20), channel_id=1, source_target_pairs={{8,0},{12,4},{16,8},{20,12},{24,16},{28,20},{32,24},{36,28},{40,32... | collective-permute-start | bytes 688136 | tf_op jit(solution)/shard_map/ppermute | solution.py:103
  162.8 24.9 %collective-permute-start.2 = (bf16[128,896]{0,1:T(8,128)(2,1)}, bf16[128,896]{0,1:T(8,128)(2,1)}, u32[]{:S(2)}, u32[]{:S(2)}) collective-permute-start(bf16[128,896]{0,1:T(8,128)(2,1)} %get-tuple-element.16), channel_id=1, source_target_pairs={{120,0},{124,4},{0,8},{4,12},{8,16},{12,20},{16,24},{20,28},{24,32... | collective-permute-start | bytes 688136 | tf_op jit(solution)/shard_map/ppermute | solution.py:103
  166.3 22.4 %collective-permute-start.3 = (bf16[128,896]{0,1:T(8,128)(2,1)}, bf16[128,896]{0,1:T(8,128)(2,1)}, u32[]{:S(2)}, u32[]{:S(2)}) collective-permute-start(bf16[128,896]{0,1:T(8,128)(2,1)} %get-tuple-element.17), channel_id=1, source_target_pairs={{128,0},{132,4},{136,8},{140,12},{144,16},{148,20},{152,24},{156,2... | collective-permute-start | bytes 688136 | tf_op jit(solution)/shard_map/ppermute | solution.py:103
  169.6 20.1 %collective-permute-start.4 = (bf16[128,896]{0,1:T(8,128)(2,1)}, bf16[128,896]{0,1:T(8,128)(2,1)}, u32[]{:S(2)}, u32[]{:S(2)}) collective-permute-start(bf16[128,896]{0,1:T(8,128)(2,1)} %get-tuple-element.18), channel_id=1, source_target_pairs={{384,0},{388,4},{392,8},{396,12},{400,16},{404,20},{408,24},{412,2... | collective-permute-start | bytes 688136 | tf_op jit(solution)/shard_map/ppermute | solution.py:103
  175.5 6.2 %copy-start.7 = (bf16[128,896]{0,1:T(8,128)(2,1)S(1)}, bf16[128,896]{0,1:T(8,128)(2,1)}, u32[]{:S(2)}) copy-start(bf16[128,896]{0,1:T(8,128)(2,1)} %get-tuple-element.15) | copy-start | bytes 688132
  181.7 10.0 %collective-permute-start.5 = (bf16[128,896]{0,1:T(8,128)(2,1)S(1)}, bf16[128,896]{0,1:T(8,128)(2,1)S(1)}, u32[]{:S(2)}, u32[]{:S(2)}) collective-permute-start(bf16[128,896]{0,1:T(8,128)(2,1)S(1)} %copy-done.7), channel_id=1, source_target_pairs={{12,0},{8,4},{20,8},{16,12},{28,16},{24,20},{36,24},{32,28},{44,32... | collective-permute-start | bytes 688136 | tf_op jit(solution)/shard_map/ppermute | solution.py:103
  194.3 3.6 copy-start.3
  297.3 1.9 copy-start.2
  299.3 1.5 copy-start.9
  304.0 22.6 %collective-permute-start.10 = (bf16[128,896]{0,1:T(8,128)(2,1)S(1)}, bf16[128,896]{0,1:T(8,128)(2,1)S(1)}, u32[]{:S(2)}, u32[]{:S(2)}) collective-permute-start(bf16[128,896]{0,1:T(8,128)(2,1)S(1)} %get-tuple-element.22), channel_id=1, source_target_pairs={{0,8},{4,12},{8,16},{12,20},{16,24},{20,28},{24,32},{28,36},{32,40... | collective-permute-start | bytes 688136 | tf_op jit(solution)/shard_map/ppermute | solution.py:118
  310.7 24.6 %collective-permute-start.11 = (bf16[128,896]{0,1:T(8,128)(2,1)}, bf16[128,896]{0,1:T(8,128)(2,1)}, u32[]{:S(2)}, u32[]{:S(2)}) collective-permute-start(bf16[128,896]{0,1:T(8,128)(2,1)} %get-tuple-element.21), channel_id=1, source_target_pairs={{0,4},{4,0},{8,12},{12,8},{16,20},{20,16},{24,28},{28,24},{32,36},... | collective-permute-start | bytes 688136 | tf_op jit(solution)/shard_map/ppermute | solution.py:118
  315.5 19.9 %collective-permute-start.6 = (bf16[128,896]{0,1:T(8,128)(2,1)}, bf16[128,896]{0,1:T(8,128)(2,1)}, u32[]{:S(2)}, u32[]{:S(2)}) collective-permute-start(bf16[128,896]{0,1:T(8,128)(2,1)} %get-tuple-element.26), channel_id=1, source_target_pairs={{0,12},{4,8},{8,20},{12,16},{16,28},{20,24},{24,36},{28,32},{32,44... | collective-permute-start | bytes 688136 | tf_op jit(solution)/shard_map/ppermute | solution.py:118
  319.2 16.2 %collective-permute-start.7 = (bf16[128,896]{0,1:T(8,128)(2,1)}, bf16[128,896]{0,1:T(8,128)(2,1)}, u32[]{:S(2)}, u32[]{:S(2)}) collective-permute-start(bf16[128,896]{0,1:T(8,128)(2,1)} %get-tuple-element.25), channel_id=1, source_target_pairs={{0,384},{4,388},{8,392},{12,396},{16,400},{20,404},{24,408},{28,41... | collective-permute-start | bytes 688136 | tf_op jit(solution)/shard_map/ppermute | solution.py:118
  324.3 4.3 slice-start
  324.4 4.3 copy-start.10
  324.4 11.0 %collective-permute-start.8 = (bf16[128,896]{0,1:T(8,128)(2,1)}, bf16[128,896]{0,1:T(8,128)(2,1)}, u32[]{:S(2)}, u32[]{:S(2)}) collective-permute-start(bf16[128,896]{0,1:T(8,128)(2,1)} %get-tuple-element.24), channel_id=1, source_target_pairs={{0,128},{4,132},{8,136},{12,140},{16,144},{20,148},{24,152},{28,15... | collective-permute-start | bytes 688136 | tf_op jit(solution)/shard_map/ppermute | solution.py:118
  326.6 2.0 copy-start.4
  326.6 9.0 %collective-permute-start.9 = (bf16[128,896]{0,1:T(8,128)(2,1)}, bf16[128,896]{0,1:T(8,128)(2,1)}, u32[]{:S(2)}, u32[]{:S(2)}) collective-permute-start(bf16[128,896]{0,1:T(8,128)(2,1)} %get-tuple-element.23), channel_id=1, source_target_pairs={{0,120},{4,124},{8,0},{12,4},{16,8},{20,12},{24,16},{28,20},{32,24... | collective-permute-start | bytes 688136 | tf_op jit(solution)/shard_map/ppermute | solution.py:118
  335.3 0.9 copy-start.5
  342.5 10.9 %copy-start.8 = (f32[128,8]{0,1:T(8,128)S(1)}, f32[128,8]{0,1:T(8,128)}, u32[]{:S(2)}) copy-start(f32[128,8]{0,1:T(8,128)} %param.7) | copy-start | bytes 12292
  342.5 120.6 %all-to-all-start.3 = ((bf16[128,8,1120]{2,1,0:T(8,128)(2,1)}), bf16[128,8,1120]{2,1,0:T(8,128)(2,1)}, u32[]{:S(2)}, u32[]{:S(2)}) async-start(bf16[128,8,1120]{2,1,0:T(8,128)(2,1)} %copy.69), calls=%async_computation.3 | async-start | bytes 4718592 | tf_op jit(solution)/shard_map/all_to_all | solution.py:29
  463.1 10.2 %copy-start.1 = (bf16[1,896,1024]{2,1,0:T(8,128)(2,1)S(1)}, bf16[1,896,1024]{2,1,0:T(8,128)(2,1)}, u32[]{:S(2)}) copy-start(bf16[1,896,1024]{2,1,0:T(8,128)(2,1)} %param.8) | copy-start | bytes 5505028
